TPU v7x, 256 devices: a whole 4x4x8 slice. The times are simulated.
256 devices in a mesh: row: 8 (over y, x_lo), col: 32 (over x_hi, z, core).
Axes of the slice: x: 4 (x_hi: 2, x_lo: 2; x = x_hi * 2 + x_lo), y: 4, z: 8, core: 2. Of those that a mesh axis runs over, the one named last changes fastest.
Arguments:
- vectors: bfloat16 [16, 131072], P(None, ('row', 'col')), may hold values from -6 to 6
- blocks: bfloat16 [8, 6144, 128, 128], P('row', 'col'), may hold values from -0.09375 to 0.09375
- row_ptr: int32 [8, 4128], P('row', 'col'), may hold values from 0 to 192, as said below
- col_idx: int32 [8, 6144], P('row', 'col'), may hold values from 0 to 31, as said below
Outputs:
- product: float32 [16, 131072], P(None, ('row', 'col'))
Inputs may be any that keep to these rules, and one draw needn't show every extreme that they name: For each tile, row_ptr starts at 0, never falls, and ends at the tile's count of live slots; at least one tile has exactly 192 live slots in every draw, and counts differ strongly from tile to tile. `col_idx`: within each block row of a tile the live slots name strictly rising block columns, so no block position of a tile is stored twice; slots at or past a tile's count hold a valid column and are unused.
All inputs are finite; a program needn't handle non-finite values.
Results may differ from a plain program's by a relative error of at most 0.0003.
Values may be sent and summed in bfloat16 or wider, within the bound.
No kernel may reach another device: no remote copies, remote signals or barrier semaphores. Data moves between devices by JAX's collectives and lax.ppermute only.
A program may use at most 64 MiB of HBM per device.

v0:
```python
import jax
import jax.numpy as jnp
from jax import lax
from jax.sharding import PartitionSpec as P


def tile_terms(row_side, col_side, tile_blocks, pointers, columns):
    slot_ids = jnp.arange(tile_blocks.shape[0], dtype=jnp.int32)
    live_slots = slot_ids < pointers[-1]
    slot_rows = jnp.sum((slot_ids[:, None] >= pointers[None, 1:]).astype(jnp.int32), axis=1)
    slot_rows = jnp.minimum(slot_rows, pointers.shape[0] - 2)
    count_vectors = row_side.shape[0]
    edge = tile_blocks.shape[1]
    row_blocks = row_side.reshape(count_vectors, -1, edge)
    col_blocks = col_side.reshape(count_vectors, -1, edge)
    picked_rows = jnp.take(row_blocks, slot_rows, axis=1)
    picked_cols = jnp.take(col_blocks, columns, axis=1)
    forward = jnp.einsum(
        "ksj,sij->ski", picked_cols, tile_blocks, preferred_element_type=jnp.float32
    )
    backward = jnp.einsum(
        "ksi,sij->skj", picked_rows, tile_blocks, preferred_element_type=jnp.float32
    )
    live_mask = live_slots[:, None, None]
    forward = jnp.where(live_mask, forward, jnp.zeros_like(forward))
    backward = jnp.where(live_mask, backward, jnp.zeros_like(backward))
    forward_sum = jax.ops.segment_sum(
        forward, slot_rows, num_segments=row_blocks.shape[1], indices_are_sorted=True
    )
    backward_sum = jax.ops.segment_sum(backward, columns, num_segments=col_blocks.shape[1])
    return (forward_sum, backward_sum)


def body(vectors, blocks, row_ptr, col_idx):
    count_vectors = vectors.shape[0]
    segment = vectors.shape[1]
    grid_rows = lax.axis_size("row")
    grid_cols = lax.axis_size("col")
    everything = lax.all_gather(vectors, ("row", "col"), axis=1, tiled=True)
    row_side = lax.dynamic_slice_in_dim(
        everything, lax.axis_index("row") * (grid_cols * segment), grid_cols * segment, 1
    )
    spread = everything.reshape(count_vectors, grid_rows, grid_cols, segment)
    col_side = lax.dynamic_slice_in_dim(spread, lax.axis_index("col"), 1, 2).reshape(
        count_vectors, grid_rows * segment
    )
    forward_sum, backward_sum = tile_terms(row_side, col_side, blocks[0], row_ptr[0], col_idx[0])
    forward_part = lax.psum_scatter(forward_sum, "col", scatter_dimension=0, tiled=True)
    backward_part = lax.psum_scatter(backward_sum, "row", scatter_dimension=0, tiled=True)
    combined = forward_part + backward_part
    return combined.transpose(1, 0, 2).reshape(count_vectors, segment)


def solution(mesh):
    in_specs = (
        P(None, ("row", "col")),
        P("row", "col", None, None),
        P("row", "col"),
        P("row", "col"),
    )
    out_specs = P(None, ("row", "col"))
    return jax.shard_map(body, mesh=mesh, in_specs=in_specs, out_specs=out_specs, check_vma=False)
```

profile of v0, /device:TPU:8, one launch (start us, length us, event | category | flops | bytes accessed | tf_op | source)
XLA Modules:
  0.0 608.5 jit_solution(9309983485756426636)
XLA Ops:
  6.5 0.0 all-gather.2.cloned.1.call-start
  6.5 0.7 all-gather.2.cloned.1.call-update
  7.3 0.0 reduce-scatter.5.cloned.1.call-start
  7.3 1.2 slice.9
  8.5 0.6 iota_compare_fusion.1
  9.1 0.8 slice_bitcast_fusion
  9.9 0.1 convert_reduce_fusion
  10.1 0.7 compare_and_fusion.1
  10.7 0.7 compare_select_fusion.1
  11.4 413.9 %all-gather.2.cloned.1.call-done = bf16[16,131072]{1,0:T(8,128)(2,1)} async-done(((bf16[16,512]{1,0:T(8,128)(2,1)}), bf16[16,131072]{1,0:T(8,128)(2,1)}) %all-gather.2.cloned.1.call-update) | async-done | bytes 4194320 | tf_op jit(solution)/shard_map/all_gather | solution.py:39
  425.3 1.1 copy_bitcast_fusion
  426.4 0.8 gather_fusion.1
  427.2 0.0 copy-start.2
  427.2 4.2 fusion.7
  431.5 0.0 copy-done.2
  431.5 7.6 %scatter_fusion.1 = f32[32,16,128]{2,1,0:T(8,128)S(1)} fusion(f32[32,16,128]{2,1,0:T(8,128)S(1)} %broadcast_in_dim.43, s32[192]{0:T(256)S(1)} %bitcast.42, f32[192,16,128]{2,1,0:T(8,128)S(1)} %fusion.7), kind=kCustom, calls=%fused_computation.3 | custom fusion | flops 393216 | bytes 4719360 | tf_op jit(solution)/shard_map/scatter-add | solution.py:30
  439.1 0.7 copy-done
  439.8 0.0 reduce-scatter.5.cloned.1.call-update
  439.8 0.0 reduce-scatter.3.cloned.1.call-start
  439.9 3.6 copy.18
  443.5 0.8 dynamic-slice_reduce_fusion
  444.3 0.1 reshape_reshape.3
  444.4 0.1 copy.12
  444.4 0.8 gather_fusion
  445.2 5.8 fusion.4
  451.0 0.1 broadcast_in_dim.39
  451.1 7.8 %scatter_fusion = f32[128,16,128]{2,1,0:T(8,128)S(1)} fusion(f32[128,16,128]{2,1,0:T(8,128)S(1)} %broadcast_in_dim.39, s32[192]{0:T(256)S(1)} %broadcast_minimum_fusion, f32[192,16,128]{2,1,0:T(8,128)S(1)} %fusion.4), kind=kCustom, calls=%fused_computation.2 | custom fusion | flops 393216 | bytes 4719360 | tf_op jit(solution)/shard_map/scatter-add | solution.py:27
  459.0 1.0 copy-done.1
  460.0 0.0 reduce-scatter.3.cloned.1.call-update
  460.0 19.8 %reduce-scatter.5.cloned.1.call-done = f32[4,16,128]{2,1,0:T(8,128)} async-done(((f32[32,16,128]{2,1,0:T(8,128)}), f32[4,16,128]{2,1,0:T(8,128)}) %reduce-scatter.5.cloned.1.call-update) | async-done | bytes 32784 | tf_op jit(solution)/shard_map/reduce_scatter | solution.py:49
  479.8 120.8 %reduce-scatter.3.cloned.1.call-done = f32[4,16,128]{2,1,0:T(8,128)} async-done(((f32[128,16,128]{2,1,0:T(8,128)}), f32[4,16,128]{2,1,0:T(8,128)}) %reduce-scatter.3.cloned.1.call-update) | async-done | bytes 32784 | tf_op jit(solution)/shard_map/reduce_scatter | solution.py:48
  600.5 1.4 copy_bitcast_fusion.1
  (8 shorter events, 0.1 us)
Async XLA Ops:
  6.5 418.8 %all-gather.2.cloned.1.call-start = ((), (), s32[]{:S(2)}) async-start(), calls=%async_computation.2 | async-start | bytes 4210688 | tf_op jit(solution)/shard_map/all_gather | solution.py:39
  7.3 472.5 %reduce-scatter.5.cloned.1.call-start = ((), (), s32[]{:S(2)}) async-start(), calls=%async_computation.4 | async-start | bytes 294912 | tf_op jit(solution)/shard_map/reduce_scatter | solution.py:49
  427.2 4.3 copy-start.2
  439.1 0.7 copy-start
  439.8 160.7 %reduce-scatter.3.cloned.1.call-start = ((), (), s32[]{:S(2)}) async-start(), calls=%async_computation.3 | async-start | bytes 1081344 | tf_op jit(solution)/shard_map/reduce_scatter | solution.py:48
  459.0 1.0 copy-start.1
Sparse Core Ops, SparseCore 0:
  9.2 416.0 all-gather.1
  439.9 39.8 reduce-scatter.4
  483.9 116.6 reduce-scatter.2
where the time goes:
time: 609 us; the launch traced here: 608 us
  waiting for transfers between devices  555 us (91%)
  other arithmetic  19 us (3%)
  between operations  13.3 us (2%)
  local copies, waits for them, and re-layouts  10.9 us (2%)
  matrix products  10.1 us (2%)
    all_gather x1, waiting for transfers between devices, body(): everything = lax.all_gather(vectors, ('row', 'col'), axis=1, tiled=True)  414 us
    reduce_scatter x1, waiting for transfers between devices, body(): lax.psum_scatter(forward_sum, 'col', scatter_dimension=0, tiled=True)  121 us
    reduce_scatter x1, waiting for transfers between devices, body(): lax.psum_scatter(backward_sum, 'row', scatter_dimension=0, tiled=True)  19.8 us
  transfers between devices with their start and end apart: 3, of which 3 were waited for; matrix products, arithmetic and copies ran while one was open for 4% of the time, Pallas kernels for 0%

commit v1 on v0

v1 whole, which is shorter than its diff:
```python
import functools

import jax
import jax.numpy as jnp
from jax import lax
from jax.experimental import pallas as pl
from jax.experimental.pallas import tpu as pltpu
from jax.sharding import PartitionSpec as P

GROUP = 16


def _tile_kernel(rows_ref, cols_ref, count_ref, blocks_ref, vec_ref, out_ref, *, forward):
    g = pl.program_id(0)

    @pl.when(g == 0)
    def _():
        out_ref[...] = jnp.zeros_like(out_ref)

    count = count_ref[0]

    def step(t, carry):
        s = g * GROUP + t
        i = rows_ref[s]
        q = cols_ref[s]
        blk = blocks_ref[t]

        @pl.when(s < count)
        def _():
            if forward:
                part = lax.dot_general(
                    vec_ref[q], blk, (((1,), (1,)), ((), ())), preferred_element_type=jnp.float32
                )
                out_ref[i] += part
            else:
                part = jnp.dot(vec_ref[i], blk, preferred_element_type=jnp.float32)
                out_ref[q] += part

        return carry

    lax.fori_loop(0, GROUP, step, 0, unroll=True)


def tile_apply(slot_rows, columns, count, blocks, vec_blocks, out_blocks, forward):
    slots, edge, _ = blocks.shape
    count_vectors = vec_blocks.shape[1]
    kernel = functools.partial(_tile_kernel, forward=forward)
    grid_spec = pltpu.PrefetchScalarGridSpec(
        num_scalar_prefetch=3,
        grid=(slots // GROUP,),
        in_specs=[
            pl.BlockSpec((GROUP, edge, edge), lambda g, *_: (g, 0, 0)),
            pl.BlockSpec(vec_blocks.shape, lambda g, *_: (0, 0, 0)),
        ],
        out_specs=pl.BlockSpec((out_blocks, count_vectors, edge), lambda g, *_: (0, 0, 0)),
    )
    return pl.pallas_call(
        kernel,
        grid_spec=grid_spec,
        out_shape=jax.ShapeDtypeStruct((out_blocks, count_vectors, edge), jnp.float32),
        compiler_params=pltpu.CompilerParams(dimension_semantics=("arbitrary",)),
        cost_estimate=pl.CostEstimate(
            flops=2 * slots * count_vectors * edge * edge,
            transcendentals=0,
            bytes_accessed=slots * edge * edge * 2 + out_blocks * count_vectors * edge * 4,
        ),
    )(slot_rows, columns, count, blocks, vec_blocks)


def body(vectors, blocks, row_ptr, col_idx):
    count_vectors = vectors.shape[0]
    segment = vectors.shape[1]
    tile_blocks = blocks[0]
    slots, edge, _ = tile_blocks.shape
    pointers = row_ptr[0]
    columns = col_idx[0]
    tile_rows = pointers.shape[0] - 1
    seg_blocks = segment // edge
    grid_rows = lax.axis_size("row")
    tile_cols = grid_rows * seg_blocks

    slot_ids = jnp.arange(slots, dtype=jnp.int32)
    slot_rows = jnp.sum((slot_ids[:, None] >= pointers[None, 1:]).astype(jnp.int32), axis=1)
    slot_rows = jnp.minimum(slot_rows, tile_rows - 1).astype(jnp.int32)
    columns = jnp.clip(columns, 0, tile_cols - 1).astype(jnp.int32)
    count = pointers[-1:].astype(jnp.int32)

    own = vectors.reshape(count_vectors, seg_blocks, edge).transpose(1, 0, 2)
    col_side = ag_a2a(own, "row")
    row_side = ag_a2a(own, "col")

    forward_sum = tile_apply(slot_rows, columns, count, tile_blocks, col_side, tile_rows, True)
    forward_part = rs_a2a(forward_sum, "col")
    backward_sum = tile_apply(slot_rows, columns, count, tile_blocks, row_side, tile_cols, False)
    backward_part = rs_a2a(backward_sum, "row")
    combined = forward_part + backward_part
    return combined.transpose(1, 0, 2).reshape(count_vectors, segment)


def solution(mesh):
    in_specs = (
        P(None, ("row", "col")),
        P("row", "col", None, None),
        P("row", "col"),
        P("row", "col"),
    )
    out_specs = P(None, ("row", "col"))
    return jax.shard_map(body, mesh=mesh, in_specs=in_specs, out_specs=out_specs, check_vma=False)


def ag_doubling(x, axis):
    n = lax.axis_size(axis)
    me = lax.axis_index(axis)
    buf = x
    b = 1
    while b < n:
        recv = lax.ppermute(buf, axis, [(i, i ^ b) for i in range(n)])
        low = (me & b) == 0
        buf = jnp.concatenate([jnp.where(low, buf, recv), jnp.where(low, recv, buf)], 0)
        b *= 2
    return buf


def rs_a2a(x, axis):
    n = lax.axis_size(axis)
    y = lax.all_to_all(x, axis, 0, 0, tiled=True)
    return y.reshape(n, -1, *x.shape[1:]).sum(0)


def ag_a2a(x, axis):
    n = lax.axis_size(axis)
    y = jnp.broadcast_to(x[None], (n,) + x.shape).reshape(n * x.shape[0], *x.shape[1:])
    return lax.all_to_all(y, axis, 0, 0, tiled=True)
```

time: 609 us -> 141 us (0.23)
  waiting for transfers between devices: 555 us -> 48.4 us
  starting transfers between devices: 0.08 us -> 63.1 us
  Pallas kernels: 0 us -> 20.8 us
  other arithmetic: 19 us -> 2.66 us
  between operations: 13.3 us -> 0.03 us
  matrix products: 10.1 us -> 0 us
  local copies, waits for them, and re-layouts: 10.9 us -> 4.34 us
    all_gather x1 -> x0, waiting for transfers between devices: 414 us -> none  [body(): everything = lax.all_gather(vectors, ('row', 'col'), axis=1, tiled=True)]
    reduce_scatter x2 -> x0, waiting for transfers between devices: 141 us -> none  [the longest x1 121 us: body(): lax.psum_scatter(forward_sum, 'col', scatter_dimension=0, tiled=True)]
    all_to_all x0 -> x4, starting transfers between devices: none -> 63.1 us  [the longest x2 46.8 us: rs_a2a(): y = lax.all_to_all(x, axis, 0, 0, tiled=True)]
    all_to_all x0 -> x4, waiting for transfers between devices: none -> 48.4 us  [the longest x2 30 us: rs_a2a(): y = lax.all_to_all(x, axis, 0, 0, tiled=True)]
    pallas_call x0 -> x2, Pallas kernels: none -> 20.8 us  [tile_apply(): pl.pallas_call(kernel, grid_spec=grid_spec, out_shape=jax.ShapeDtypeStruc...]
    scatter-add x2 -> x0, other arithmetic: 15.4 us -> none  [the longest x1 7.83 us: tile_terms(): jax.ops.segment_sum(forward, slot_rows, num_segments=row_blocks.shape[1],...]
    dot_general x2 -> x0, matrix products: 10.1 us -> none  [the longest x1 5.82 us: tile_terms(): jnp.einsum('ksj,sij->ski', picked_cols, tile_blocks, preferred_element_ty...]
  transfers between devices with their start and end apart: 3 -> 4, of which waited for: 3 -> 2; matrix products, arithmetic and copies ran while one was open for 4% -> 3% of each run, Pallas kernels for 0% -> 15%
where the time goes in v1:
time: 141 us; the launch traced here: 139 us
  starting transfers between devices  63.1 us (45%)
  waiting for transfers between devices  48.4 us (34%)
  Pallas kernels  20.8 us (15%)
  local copies, waits for them, and re-layouts  4.34 us (3%)
  other arithmetic  2.66 us (2%)
    all_to_all x2, starting transfers between devices, rs_a2a(): y = lax.all_to_all(x, axis, 0, 0, tiled=True)  46.8 us
    all_to_all x2, waiting for transfers between devices, rs_a2a(): y = lax.all_to_all(x, axis, 0, 0, tiled=True)  30 us
    pallas_call x2, Pallas kernels, tile_apply(): pl.pallas_call(kernel, grid_spec=grid_spec, out_shape=jax.ShapeDtypeStruc...  20.8 us
    all_to_all x2, waiting for transfers between devices, ag_a2a(): return lax.all_to_all(y, axis, 0, 0, tiled=True)  18.5 us
    all_to_all x2, starting transfers between devices, ag_a2a(): return lax.all_to_all(y, axis, 0, 0, tiled=True)  16.3 us
  transfers between devices with their start and end apart: 4, of which 2 were waited for; matrix products, arithmetic and copies ran while one was open for 3% of the time, Pallas kernels for 15%

profile of v1, /device:TPU:8, one launch (start us, length us, event | category | flops | bytes accessed | tf_op | source)
XLA Modules:
  0.0 139.3 jit_solution(3029241053686625245)
XLA Ops:
  0.0 0.7 reshape.25
  0.7 0.9 broadcast_in_dim.5
  1.6 11.3 %all-to-all-start.2 = ((bf16[128,16,128]{2,1,0:T(8,128)(2,1)}), bf16[128,16,128]{2,1,0:T(8,128)(2,1)S(1)}, u32[]{:S(2)}, u32[]{:S(2)}) async-start(bf16[128,16,128]{2,1,0:T(8,128)(2,1)} %bitcast.7), calls=%async_computation.2 | async-start | bytes 1048576 | tf_op jit(solution)/shard_map/all_to_all | solution.py:133
  13.0 0.8 slice_bitcast_fusion
  13.7 0.1 convert_reduce_fusion
  13.8 0.6 broadcast_minimum_fusion.rows_ref
  14.4 18.5 %all-to-all-done.2.vec_ref = bf16[128,16,128]{2,1,0:T(8,128)(2,1)S(1)} async-done(((bf16[128,16,128]{2,1,0:T(8,128)(2,1)}), bf16[128,16,128]{2,1,0:T(8,128)(2,1)S(1)}, u32[]{:S(2)}, u32[]{:S(2)}) %all-to-all-start.2) | async-done | bytes 524320 | tf_op jit(solution)/shard_map/all_to_all | solution.py:133
  32.9 0.0 copy-start
  32.9 0.7 broadcast_in_dim.4
  33.6 4.9 %all-to-all-start = ((bf16[32,16,128]{2,1,0:T(8,128)(2,1)}), bf16[32,16,128]{2,1,0:T(8,128)(2,1)S(1)}, u32[]{:S(2)}, u32[]{:S(2)}) async-start(bf16[32,16,128]{2,1,0:T(8,128)(2,1)} %bitcast.5), calls=%async_computation | async-start | bytes 262144 | tf_op jit(solution)/shard_map/all_to_all | solution.py:133
  38.6 1.3 broadcast_clamp_fusion
  39.8 1.2 slice.11
  41.0 0.0 copy-done
  41.0 10.3 %shard_map.47 = f32[32,16,128]{2,1,0:T(8,128)} custom-call(s32[192]{0:T(256)} %broadcast_minimum_fusion.rows_ref, s32[192]{0:T(256)} %bitcast.21, s32[1]{0:T(128)} %bitcast.2.count_ref, bf16[192,128,128]{2,1,0:T(8,128)(2,1)} %bitcast.16, bf16[128,16,128]{2,1,0:T(8,128)(2,1)} %copy-done), custom_call_target="tpu_custom_call" | custom-call | flops 100663296 | bytes 6553600 | tf_op jit(solution)/shard_map/pallas_call | solution.py:57
  51.3 0.0 all-to-all-done.vec_ref
  51.3 0.0 copy-start.1
  51.3 21.5 %all-to-all-start.3 = ((f32[32,16,128]{2,1,0:T(8,128)}), f32[32,16,128]{2,1,0:T(8,128)S(1)}, u32[]{:S(2)}, u32[]{:S(2)}) async-start(f32[32,16,128]{2,1,0:T(8,128)} %shard_map.47), calls=%async_computation.3 | async-start | bytes 524288 | tf_op jit(solution)/shard_map/all_to_all | solution.py:126
  72.8 0.0 copy-done.1
  72.8 10.5 %shard_map.46 = f32[128,16,128]{2,1,0:T(8,128)} custom-call(s32[192]{0:T(256)} %broadcast_minimum_fusion.rows_ref, s32[192]{0:T(256)} %bitcast.22, s32[1]{0:T(128)} %bitcast.2.count_ref, bf16[192,128,128]{2,1,0:T(8,128)(2,1)} %bitcast.17, bf16[32,16,128]{2,1,0:T(8,128)(2,1)} %copy-done.1), custom_call_target="tpu_custom_call" | custom-call | flops 100663296 | bytes 7340032 | tf_op jit(solution)/shard_map/pallas_call | solution.py:57
  83.3 0.0 all-to-all-done.3
  83.3 25.4 %all-to-all-start.1 = ((f32[128,16,128]{2,1,0:T(8,128)}), f32[128,16,128]{2,1,0:T(8,128)S(1)}, u32[]{:S(2)}, u32[]{:S(2)}) async-start(f32[128,16,128]{2,1,0:T(8,128)} %shard_map.46), calls=%async_computation.1 | async-start | bytes 2097152 | tf_op jit(solution)/shard_map/all_to_all | solution.py:126
  108.7 30.0 %all-to-all-done.1 = f32[128,16,128]{2,1,0:T(8,128)S(1)} async-done(((f32[128,16,128]{2,1,0:T(8,128)}), f32[128,16,128]{2,1,0:T(8,128)S(1)}, u32[]{:S(2)}, u32[]{:S(2)}) %all-to-all-start.1) | async-done | bytes 1048608 | tf_op jit(solution)/shard_map/all_to_all | solution.py:126
  138.7 0.1 reduce_sum.28
  138.7 0.6 copy_bitcast_fusion
  (2 shorter events, 0.0 us)
Async XLA Ops:
  1.6 31.2 %all-to-all-start.2 = ((bf16[128,16,128]{2,1,0:T(8,128)(2,1)}), bf16[128,16,128]{2,1,0:T(8,128)(2,1)S(1)}, u32[]{:S(2)}, u32[]{:S(2)}) async-start(bf16[128,16,128]{2,1,0:T(8,128)(2,1)} %bitcast.7), calls=%async_computation.2 | async-start | bytes 1048576 | tf_op jit(solution)/shard_map/all_to_all | solution.py:133
  32.9 8.2 %copy-start = (bf16[128,16,128]{2,1,0:T(8,128)(2,1)}, bf16[128,16,128]{2,1,0:T(8,128)(2,1)S(1)}, u32[]{:S(2)}) copy-start(bf16[128,16,128]{2,1,0:T(8,128)(2,1)S(1)} %all-to-all-done.2.vec_ref) | copy-start | bytes 1572868
  33.6 17.7 %all-to-all-start = ((bf16[32,16,128]{2,1,0:T(8,128)(2,1)}), bf16[32,16,128]{2,1,0:T(8,128)(2,1)S(1)}, u32[]{:S(2)}, u32[]{:S(2)}) async-start(bf16[32,16,128]{2,1,0:T(8,128)(2,1)} %bitcast.5), calls=%async_computation | async-start | bytes 262144 | tf_op jit(solution)/shard_map/all_to_all | solution.py:133
  51.3 21.5 %copy-start.1 = (bf16[32,16,128]{2,1,0:T(8,128)(2,1)}, bf16[32,16,128]{2,1,0:T(8,128)(2,1)S(1)}, u32[]{:S(2)}) copy-start(bf16[32,16,128]{2,1,0:T(8,128)(2,1)S(1)} %all-to-all-done.vec_ref) | copy-start | bytes 393220
  51.3 32.0 %all-to-all-start.3 = ((f32[32,16,128]{2,1,0:T(8,128)}), f32[32,16,128]{2,1,0:T(8,128)S(1)}, u32[]{:S(2)}, u32[]{:S(2)}) async-start(f32[32,16,128]{2,1,0:T(8,128)} %shard_map.47), calls=%async_computation.3 | async-start | bytes 524288 | tf_op jit(solution)/shard_map/all_to_all | solution.py:126
  83.3 55.4 %all-to-all-start.1 = ((f32[128,16,128]{2,1,0:T(8,128)}), f32[128,16,128]{2,1,0:T(8,128)S(1)}, u32[]{:S(2)}, u32[]{:S(2)}) async-start(f32[128,16,128]{2,1,0:T(8,128)} %shard_map.46), calls=%async_computation.1 | async-start | bytes 2097152 | tf_op jit(solution)/shard_map/all_to_all | solution.py:126

commit v2 on v1

--- a/solution.py
+++ b/solution.py
@@ -18,27 +18,22 @@
         out_ref[...] = jnp.zeros_like(out_ref)
 
     count = count_ref[0]
-
-    def step(t, carry):
+    parts = []
+    for t in range(GROUP):
         s = g * GROUP + t
-        i = rows_ref[s]
-        q = cols_ref[s]
         blk = blocks_ref[t]
-
-        @pl.when(s < count)
-        def _():
-            if forward:
-                part = lax.dot_general(
-                    vec_ref[q], blk, (((1,), (1,)), ((), ())), preferred_element_type=jnp.float32
-                )
-                out_ref[i] += part
-            else:
-                part = jnp.dot(vec_ref[i], blk, preferred_element_type=jnp.float32)
-                out_ref[q] += part
-
-        return carry
-
-    lax.fori_loop(0, GROUP, step, 0, unroll=True)
+        if forward:
+            part = lax.dot_general(
+                vec_ref[cols_ref[s]], blk, (((1,), (1,)), ((), ())),
+                preferred_element_type=jnp.float32,
+            )
+        else:
+            part = jnp.dot(vec_ref[rows_ref[s]], blk, preferred_element_type=jnp.float32)
+        parts.append(jnp.where(s < count, part, jnp.zeros_like(part)))
+    for t in range(GROUP):
+        s = g * GROUP + t
+        target = rows_ref[s] if forward else cols_ref[s]
+        out_ref[target] += parts[t]
 
 
 def tile_apply(slot_rows, columns, count, blocks, vec_blocks, out_blocks, forward):
@@ -67,6 +62,37 @@
     )(slot_rows, columns, count, blocks, vec_blocks)
 
 
+def _bits(n):
+    bits = n.bit_length() - 1
+    assert 1 << bits == n
+    return bits
+
+
+def gather_blocks(own, axis):
+    n = lax.axis_size(axis)
+    me = lax.axis_index(axis)
+    buf = own[None]
+    for b in reversed(range(_bits(n))):
+        recv = lax.ppermute(buf, axis, [(i, i ^ (1 << b)) for i in range(n)])
+        low = ((me >> b) & 1) == 0
+        buf = jnp.where(low, jnp.stack([buf, recv], 1), jnp.stack([recv, buf], 1))
+        buf = buf.reshape(-1, *own.shape)
+    return buf.reshape(n * own.shape[0], *own.shape[1:])
+
+
+def scatter_sum(x, axis, seg_blocks):
+    n = lax.axis_size(axis)
+    me = lax.axis_index(axis)
+    buf = x.reshape(n, seg_blocks, *x.shape[1:])
+    for b in range(_bits(n)):
+        buf = buf.reshape(-1, 2, *buf.shape[1:])
+        bit = (me >> b) & 1
+        keep = lax.dynamic_index_in_dim(buf, bit, 1, keepdims=False)
+        send = lax.dynamic_index_in_dim(buf, 1 - bit, 1, keepdims=False)
+        buf = keep + lax.ppermute(send, axis, [(i, i ^ (1 << b)) for i in range(n)])
+    return buf.reshape(seg_blocks, *x.shape[1:])
+
+
 def body(vectors, blocks, row_ptr, col_idx):
     count_vectors = vectors.shape[0]
     segment = vectors.shape[1]
@@ -86,13 +112,13 @@
     count = pointers[-1:].astype(jnp.int32)
 
     own = vectors.reshape(count_vectors, seg_blocks, edge).transpose(1, 0, 2)
-    col_side = ag_a2a(own, "row")
-    row_side = ag_a2a(own, "col")
+    col_side = gather_blocks(own, "row")
+    row_side = gather_blocks(own, "col")
 
     forward_sum = tile_apply(slot_rows, columns, count, tile_blocks, col_side, tile_rows, True)
-    forward_part = rs_a2a(forward_sum, "col")
+    forward_part = scatter_sum(forward_sum, "col", seg_blocks)
     backward_sum = tile_apply(slot_rows, columns, count, tile_blocks, row_side, tile_cols, False)
-    backward_part = rs_a2a(backward_sum, "row")
+    backward_part = scatter_sum(backward_sum, "row", seg_blocks)
     combined = forward_part + backward_part
     return combined.transpose(1, 0, 2).reshape(count_vectors, segment)
 
@@ -106,28 +132,3 @@
     )
     out_specs = P(None, ("row", "col"))
     return jax.shard_map(body, mesh=mesh, in_specs=in_specs, out_specs=out_specs, check_vma=False)
-
-
-def ag_doubling(x, axis):
-    n = lax.axis_size(axis)
-    me = lax.axis_index(axis)
-    buf = x
-    b = 1
-    while b < n:
-        recv = lax.ppermute(buf, axis, [(i, i ^ b) for i in range(n)])
-        low = (me & b) == 0
-        buf = jnp.concatenate([jnp.where(low, buf, recv), jnp.where(low, recv, buf)], 0)
-        b *= 2
-    return buf
-
-
-def rs_a2a(x, axis):
-    n = lax.axis_size(axis)
-    y = lax.all_to_all(x, axis, 0, 0, tiled=True)
-    return y.reshape(n, -1, *x.shape[1:]).sum(0)
-
-
-def ag_a2a(x, axis):
-    n = lax.axis_size(axis)
-    y = jnp.broadcast_to(x[None], (n,) + x.shape).reshape(n * x.shape[0], *x.shape[1:])
-    return lax.all_to_all(y, axis, 0, 0, tiled=True)

time: 141 us -> 87.6 us (0.62)
  starting transfers between devices: 63.1 us -> 32 us
  waiting for transfers between devices: 48.4 us -> 22.1 us
  local copies, waits for them, and re-layouts: 4.34 us -> 6.41 us
    all_to_all x4 -> x0, starting transfers between devices: 63.1 us -> none  [the longest x2 46.8 us: rs_a2a(): y = lax.all_to_all(x, axis, 0, 0, tiled=True)]
    all_to_all x4 -> x0, waiting for transfers between devices: 48.4 us -> none  [the longest x2 30 us: rs_a2a(): y = lax.all_to_all(x, axis, 0, 0, tiled=True)]
    ppermute x0 -> x16, starting transfers between devices: none -> 32 us  [the longest x8 17.7 us: gather_blocks(): recv = lax.ppermute(buf, axis, [(i, i ^ 1 << b) for i in range(n)])]
    ppermute x0 -> x16, waiting for transfers between devices: none -> 22.1 us  [the longest x8 16.2 us: scatter_sum(): buf = keep + lax.ppermute(send, axis, [(i, i ^ 1 << b) for i in range(n)])]
    squeeze x0 -> x8, local copies, waits for them, and re-layouts: none -> 2.17 us  [scatter_sum(): send = lax.dynamic_index_in_dim(buf, 1 - bit, 1, keepdims=False)]
    broadcast_in_dim x2 -> x0, local copies, waits for them, and re-layouts: 1.62 us -> none  [ag_a2a(): jnp.broadcast_to(x[None], (n,) + x.shape)]
    select_n x0 -> x6, local copies, waits for them, and re-layouts: none -> 1.59 us  [gather_blocks(): buf = jnp.where(low, jnp.stack([buf, recv], 1), jnp.stack([recv, buf], 1))]
  transfers between devices with their start and end apart: 4 -> 16, of which waited for: 2 -> 10; matrix products, arithmetic and copies ran while one was open for 3% -> 10% of each run, Pallas kernels for 15% -> 25%
where the time goes in v2:
time: 87.6 us; the launch traced here: 86.8 us
  starting transfers between devices  32 us (37%)
  waiting for transfers between devices  22.1 us (25%)
  Pallas kernels  22.1 us (25%)
  local copies, waits for them, and re-layouts  6.41 us (7%)
  other arithmetic  3.97 us (5%)
    pallas_call x2, Pallas kernels, tile_apply(): pl.pallas_call(kernel, grid_spec=grid_spec, out_shape=jax.ShapeDtypeStruc...  22.1 us
    ppermute x8, starting transfers between devices, gather_blocks(): recv = lax.ppermute(buf, axis, [(i, i ^ 1 << b) for i in range(n)])  17.7 us
    ppermute x8, waiting for transfers between devices, scatter_sum(): buf = keep + lax.ppermute(send, axis, [(i, i ^ 1 << b) for i in range(n)])  16.2 us
    ppermute x8, starting transfers between devices, scatter_sum(): buf = keep + lax.ppermute(send, axis, [(i, i ^ 1 << b) for i in range(n)])  14.3 us
    ppermute x8, waiting for transfers between devices, gather_blocks(): recv = lax.ppermute(buf, axis, [(i, i ^ 1 << b) for i in range(n)])  5.97 us
    squeeze x8, local copies, waits for them, and re-layouts, scatter_sum(): send = lax.dynamic_index_in_dim(buf, 1 - bit, 1, keepdims=False)  2.17 us
  transfers between devices with their start and end apart: 16, of which 10 were waited for; matrix products, arithmetic and copies ran while one was open for 10% of the time, Pallas kernels for 25%

profile of v2, /device:TPU:8, one launch (start us, length us, event | category | flops | bytes accessed | tf_op | source)
XLA Modules:
  0.0 86.8 jit_solution(4652124293119076387)
XLA Ops:
  0.0 0.7 reshape.303
  0.7 2.3 %collective-permute-start = (bf16[1,4,16,128]{3,1,2,0:T(4,128)(2,1)S(1)}, bf16[1,4,16,128]{3,1,2,0:T(4,128)(2,1)S(1)}, u32[]{:S(2)}, u32[]{:S(2)}) collective-permute-start(bf16[1,4,16,128]{3,1,2,0:T(4,128)(2,1)S(1)} %bitcast.94), channel_id=1, source_target_pairs={{0,128},{32,160},{64,192},{96,224},{128,0},{160,32},{192,64},{224,... | collective-permute-start | bytes 49160 | tf_op jit(solution)/shard_map/ppermute | solution.py:76
  3.0 3.0 %collective-permute-start.8 = (bf16[1,4,16,128]{3,1,2,0:T(4,128)(2,1)S(1)}, bf16[1,4,16,128]{3,1,2,0:T(4,128)(2,1)S(1)}, u32[]{:S(2)}, u32[]{:S(2)}) collective-permute-start(bf16[1,4,16,128]{3,1,2,0:T(4,128)(2,1)S(1)} %bitcast.95), channel_id=1, source_target_pairs={{0,16},{1,17},{2,18},{3,19},{4,20},{5,21},{6,22},{7,23},{8,24},{9,... | collective-permute-start | bytes 49160 | tf_op jit(solution)/shard_map/ppermute | solution.py:76
  6.0 0.7 slice_bitcast_fusion
  7.5 1.3 %broadcast_clamp_fusion = s32[1,192]{1,0:T(1,128)} fusion(s32[1,192]{1,0:T(1,128)} %param.7), kind=kLoop, calls=%fused_computation.35 | loop fusion | flops 192 | bytes 1536 | tf_op jit(solution)/shard_map/jit(clip)/min | solution.py:111
  8.7 1.2 %slice.11 = s32[1,1]{1,0:T(1,128)} slice(s32[1,129]{1,0:T(1,128)} %param.6), slice={[0:1], [128:129]} | slice | bytes 8 | tf_op jit(solution)/shard_map/slice | solution.py:112
  10.0 1.4 %collective-permute-start.1 = (bf16[2,4,16,128]{3,1,2,0:T(4,128)(2,1)S(1)}, bf16[2,4,16,128]{3,1,2,0:T(4,128)(2,1)S(1)}, u32[]{:S(2)}, u32[]{:S(2)}) collective-permute-start(bf16[2,4,16,128]{3,1,2,0:T(4,128)(2,1)S(1)} %get-tuple-element.7), channel_id=1, source_target_pairs={{0,64},{32,96},{64,0},{96,32},{128,192},{160,224},{192,128},{224,1... | collective-permute-start | bytes 98312 | tf_op jit(solution)/shard_map/ppermute | solution.py:76
  11.4 7.2 %collective-permute-start.9 = (bf16[2,4,16,128]{3,1,2,0:T(4,128)(2,1)S(1)}, bf16[2,4,16,128]{3,1,2,0:T(4,128)(2,1)S(1)}, u32[]{:S(2)}, u32[]{:S(2)}) collective-permute-start(bf16[2,4,16,128]{3,1,2,0:T(4,128)(2,1)S(1)} %get-tuple-element.8), channel_id=1, source_target_pairs={{0,8},{1,9},{2,10},{3,11},{4,12},{5,13},{6,14},{7,15},{8,0},{9,1},... | collective-permute-start | bytes 98312 | tf_op jit(solution)/shard_map/ppermute | solution.py:76
  18.8 0.7 collective-permute-start.2
  19.4 1.1 %collective-permute-done.9 = bf16[2,4,16,128]{3,1,2,0:T(4,128)(2,1)S(1)} collective-permute-done((bf16[2,4,16,128]{3,1,2,0:T(4,128)(2,1)S(1)}, bf16[2,4,16,128]{3,1,2,0:T(4,128)(2,1)S(1)}, u32[]{:S(2)}, u32[]{:S(2)}) %collective-permute-start.9) | collective-permute-done | bytes 32800 | tf_op jit(solution)/shard_map/ppermute | solution.py:76
  20.6 2.1 %collective-permute-start.10 = (bf16[4,4,16,128]{3,2,1,0:T(8,128)(2,1)S(1)}, bf16[4,4,16,128]{3,2,1,0:T(8,128)(2,1)S(1)}, u32[]{:S(2)}, u32[]{:S(2)}) collective-permute-start(bf16[4,4,16,128]{3,2,1,0:T(8,128)(2,1)S(1)} %bitcast.101), channel_id=1, source_target_pairs={{0,4},{1,5},{2,6},{3,7},{4,0},{5,1},{6,2},{7,3},{8,12},{9,13},{10,... | collective-permute-start | bytes 196616 | tf_op jit(solution)/shard_map/ppermute | solution.py:76
  23.1 0.7 copy.38
  23.8 2.8 %collective-permute-done.10 = bf16[4,4,16,128]{3,2,1,0:T(8,128)(2,1)S(1)} collective-permute-done((bf16[4,4,16,128]{3,2,1,0:T(8,128)(2,1)S(1)}, bf16[4,4,16,128]{3,2,1,0:T(8,128)(2,1)S(1)}, u32[]{:S(2)}, u32[]{:S(2)}) %collective-permute-start.10) | collective-permute-done | bytes 65568 | tf_op jit(solution)/shard_map/ppermute | solution.py:76
  27.1 11.6 %shard_map.46 = f32[128,16,128]{2,1,0:T(8,128)} custom-call(s32[192]{0:T(256)} %broadcast_minimum_fusion.rows_ref, s32[192]{0:T(256)} %bitcast.112, s32[1]{0:T(128)} %bitcast.2.count_ref, bf16[192,128,128]{2,1,0:T(8,128)(2,1)} %bitcast.74, bf16[32,16,128]{2,1,0:T(8,128)(2,1)} %bitcast.87), custom_call_target="tpu_custom_call" | custom-call | flops 100663296 | bytes 7340032 | tf_op jit(solution)/shard_map/pallas_call | solution.py:52
  38.7 1.2 %dynamic-slice_bitcast_fusion = f32[16,4,16,128]{3,2,1,0:T(8,128)S(1)} fusion(f32[16,2,4,16,128]{4,3,2,1,0:T(8,128)} %bitcast.76, s32[]{:T(128)S(6)} %select_n.215), kind=kLoop, calls=%fused_computation.2 | loop fusion | bytes 1048580 | tf_op jit(solution)/shard_map/jit(dynamic_index_in_dim)/squeeze | solution.py:91
  40.6 1.6 %collective-permute-done.12 = bf16[16,4,16,128]{3,2,1,0:T(8,128)(2,1)S(1)} collective-permute-done((bf16[16,4,16,128]{3,2,1,0:T(8,128)(2,1)S(1)}, bf16[16,4,16,128]{3,2,1,0:T(8,128)(2,1)S(1)}, u32[]{:S(2)}, u32[]{:S(2)}) %collective-permute-start.12) | collective-permute-done | bytes 262176 | tf_op jit(solution)/shard_map/ppermute | solution.py:76
  42.3 0.9 %copy.45 = bf16[16,2,4,16,128]{4,3,2,1,0:T(8,128)(2,1)} copy(bf16[16,2,4,16,128]{4,3,2,0,1:T(8,128)(2,1)S(1)} %maximum_select_fusion) | data formatting | bytes 1048576 | tf_op jit(solution)/shard_map/jit(_where)/select_n | solution.py:78
  43.2 10.5 %shard_map.47 = f32[32,16,128]{2,1,0:T(8,128)} custom-call(s32[192]{0:T(256)} %broadcast_minimum_fusion.rows_ref, s32[192]{0:T(256)} %bitcast.113, s32[1]{0:T(128)} %bitcast.2.count_ref, bf16[192,128,128]{2,1,0:T(8,128)(2,1)} %bitcast.75, bf16[128,16,128]{2,1,0:T(8,128)(2,1)} %bitcast.80), custom_call_target="tpu_custom_call" | custom-call | flops 100663296 | bytes 6553600 | tf_op jit(solution)/shard_map/pallas_call | solution.py:52
  53.6 0.9 %dynamic-slice_bitcast_fusion.2 = f32[4,4,16,128]{3,2,1,0:T(8,128)S(1)} fusion(f32[4,2,4,16,128]{4,3,2,1,0:T(8,128)} %bitcast.85, s32[]{:T(128)S(6)} %select_n.244), kind=kLoop, calls=%fused_computation.10 | loop fusion | bytes 262148 | tf_op jit(solution)/shard_map/jit(dynamic_index_in_dim)/squeeze | solution.py:91
  54.6 0.7 collective-permute-start.13
  55.3 1.8 %collective-permute-start.4 = (f32[8,4,16,128]{3,2,1,0:T(8,128)S(1)}, f32[8,4,16,128]{3,2,1,0:T(8,128)S(1)}, u32[]{:S(2)}, u32[]{:S(2)}) collective-permute-start(f32[8,4,16,128]{3,2,1,0:T(8,128)S(1)} %dynamic-slice_bitcast_fusion.1), channel_id=1, source_target_pairs={{0,2},{1,3},{2,0},{3,1},{4,6},{5,7},{6,4},{7,5},{8,10},{9,11},{10,... | collective-permute-start | bytes 786440 | tf_op jit(solution)/shard_map/ppermute | solution.py:92
  57.1 3.0 %collective-permute-done.13 = f32[4,4,16,128]{3,2,1,0:T(8,128)S(1)} collective-permute-done((f32[4,4,16,128]{3,2,1,0:T(8,128)S(1)}, f32[4,4,16,128]{3,2,1,0:T(8,128)S(1)}, u32[]{:S(2)}, u32[]{:S(2)}) %collective-permute-start.13) | collective-permute-done | bytes 131104 | tf_op jit(solution)/shard_map/ppermute | solution.py:92
  60.2 0.9 %bitcast_add_fusion.2 = f32[4,4,16,128]{3,2,1,0:T(8,128)S(1)} fusion(f32[4,4,16,128]{3,2,1,0:T(8,128)S(1)} %collective-permute-done.13, f32[4,2,4,16,128]{4,3,2,1,0:T(8,128)} %bitcast.86, s32[]{:T(128)S(6)} %select_n.243), kind=kLoop, calls=%fused_computation.8 | loop fusion | flops 32768 | bytes 393220 | tf_op jit(solution)/shard_map/add | solution.py:92
  61.1 0.8 collective-permute-start.14
  61.9 1.6 %collective-permute-done.4 = f32[8,4,16,128]{3,2,1,0:T(8,128)S(1)} collective-permute-done((f32[8,4,16,128]{3,2,1,0:T(8,128)S(1)}, f32[8,4,16,128]{3,2,1,0:T(8,128)S(1)}, u32[]{:S(2)}, u32[]{:S(2)}) %collective-permute-start.4) | collective-permute-done | bytes 262176 | tf_op jit(solution)/shard_map/ppermute | solution.py:92
  63.6 3.2 %collective-permute-start.5 = (f32[4,4,16,128]{3,2,1,0:T(8,128)S(1)}, f32[4,4,16,128]{3,2,1,0:T(8,128)S(1)}, u32[]{:S(2)}, u32[]{:S(2)}) collective-permute-start(f32[4,4,16,128]{3,2,1,0:T(8,128)S(1)} %dynamic-slice_bitcast_fusion.3), channel_id=1, source_target_pairs={{0,4},{1,5},{2,6},{3,7},{4,0},{5,1},{6,2},{7,3},{8,12},{9,13},{10,... | collective-permute-start | bytes 393224 | tf_op jit(solution)/shard_map/ppermute | solution.py:92
  66.8 5.5 %collective-permute-done.5 = f32[4,4,16,128]{3,2,1,0:T(8,128)S(1)} collective-permute-done((f32[4,4,16,128]{3,2,1,0:T(8,128)S(1)}, f32[4,4,16,128]{3,2,1,0:T(8,128)S(1)}, u32[]{:S(2)}, u32[]{:S(2)}) %collective-permute-start.5) | collective-permute-done | bytes 131104 | tf_op jit(solution)/shard_map/ppermute | solution.py:92
  72.3 5.6 %collective-permute-start.6 = (f32[2,4,16,128]{3,2,1,0:T(8,128)S(1)}, f32[2,4,16,128]{3,2,1,0:T(8,128)S(1)}, u32[]{:S(2)}, u32[]{:S(2)}) collective-permute-start(f32[2,4,16,128]{3,2,1,0:T(8,128)S(1)} %dynamic-slice_bitcast_fusion.5), channel_id=1, source_target_pairs={{0,8},{1,9},{2,10},{3,11},{4,12},{5,13},{6,14},{7,15},{8,0},{9,1},... | collective-permute-start | bytes 196616 | tf_op jit(solution)/shard_map/ppermute | solution.py:92
  78.0 2.7 %collective-permute-done.6 = f32[2,4,16,128]{3,2,1,0:T(8,128)S(1)} collective-permute-done((f32[2,4,16,128]{3,2,1,0:T(8,128)S(1)}, f32[2,4,16,128]{3,2,1,0:T(8,128)S(1)}, u32[]{:S(2)}, u32[]{:S(2)}) %collective-permute-start.6) | collective-permute-done | bytes 65568 | tf_op jit(solution)/shard_map/ppermute | solution.py:92
  80.7 2.1 %collective-permute-start.7 = (f32[1,4,16,128]{3,2,1,0:T(8,128)S(1)}, f32[1,4,16,128]{3,2,1,0:T(8,128)S(1)}, u32[]{:S(2)}, u32[]{:S(2)}) collective-permute-start(f32[1,4,16,128]{3,2,1,0:T(8,128)S(1)} %constant_dynamic-slice_fusion), channel_id=1, source_target_pairs={{0,16},{1,17},{2,18},{3,19},{4,20},{5,21},{6,22},{7,23},{8,24},{9,... | collective-permute-start | bytes 98312 | tf_op jit(solution)/shard_map/ppermute | solution.py:92
  83.4 2.8 %collective-permute-done.7 = f32[1,4,16,128]{3,2,1,0:T(8,128)S(1)} collective-permute-done((f32[1,4,16,128]{3,2,1,0:T(8,128)S(1)}, f32[1,4,16,128]{3,2,1,0:T(8,128)S(1)}, u32[]{:S(2)}, u32[]{:S(2)}) %collective-permute-start.7) | collective-permute-done | bytes 32800 | tf_op jit(solution)/shard_map/ppermute | solution.py:92
  86.2 0.6 copy_bitcast_fusion
  (39 shorter events, 3.4 us)
Async XLA Ops:
  0.7 9.2 %collective-permute-start = (bf16[1,4,16,128]{3,1,2,0:T(4,128)(2,1)S(1)}, bf16[1,4,16,128]{3,1,2,0:T(4,128)(2,1)S(1)}, u32[]{:S(2)}, u32[]{:S(2)}) collective-permute-start(bf16[1,4,16,128]{3,1,2,0:T(4,128)(2,1)S(1)} %bitcast.94), channel_id=1, source_target_pairs={{0,128},{32,160},{64,192},{96,224},{128,0},{160,32},{192,64},{224,... | collective-permute-start | bytes 49160 | tf_op jit(solution)/shard_map/ppermute | solution.py:76
  3.0 6.9 %collective-permute-start.8 = (bf16[1,4,16,128]{3,1,2,0:T(4,128)(2,1)S(1)}, bf16[1,4,16,128]{3,1,2,0:T(4,128)(2,1)S(1)}, u32[]{:S(2)}, u32[]{:S(2)}) collective-permute-start(bf16[1,4,16,128]{3,1,2,0:T(4,128)(2,1)S(1)} %bitcast.95), channel_id=1, source_target_pairs={{0,16},{1,17},{2,18},{3,19},{4,20},{5,21},{6,22},{7,23},{8,24},{9,... | collective-permute-start | bytes 49160 | tf_op jit(solution)/shard_map/ppermute | solution.py:76
  10.0 8.7 %collective-permute-start.1 = (bf16[2,4,16,128]{3,1,2,0:T(4,128)(2,1)S(1)}, bf16[2,4,16,128]{3,1,2,0:T(4,128)(2,1)S(1)}, u32[]{:S(2)}, u32[]{:S(2)}) collective-permute-start(bf16[2,4,16,128]{3,1,2,0:T(4,128)(2,1)S(1)} %get-tuple-element.7), channel_id=1, source_target_pairs={{0,64},{32,96},{64,0},{96,32},{128,192},{160,224},{192,128},{224,1... | collective-permute-start | bytes 98312 | tf_op jit(solution)/shard_map/ppermute | solution.py:76
  11.4 9.1 %collective-permute-start.9 = (bf16[2,4,16,128]{3,1,2,0:T(4,128)(2,1)S(1)}, bf16[2,4,16,128]{3,1,2,0:T(4,128)(2,1)S(1)}, u32[]{:S(2)}, u32[]{:S(2)}) collective-permute-start(bf16[2,4,16,128]{3,1,2,0:T(4,128)(2,1)S(1)} %get-tuple-element.8), channel_id=1, source_target_pairs={{0,8},{1,9},{2,10},{3,11},{4,12},{5,13},{6,14},{7,15},{8,0},{9,1},... | collective-permute-start | bytes 98312 | tf_op jit(solution)/shard_map/ppermute | solution.py:76
  18.8 4.4 %collective-permute-start.2 = (bf16[4,4,16,128]{3,2,1,0:T(8,128)(2,1)S(1)}, bf16[4,4,16,128]{3,2,1,0:T(8,128)(2,1)S(1)}, u32[]{:S(2)}, u32[]{:S(2)}) collective-permute-start(bf16[4,4,16,128]{3,2,1,0:T(8,128)(2,1)S(1)} %bitcast.99), channel_id=1, source_target_pairs={{0,32},{32,0},{64,96},{96,64},{128,160},{160,128},{192,224},{224,1... | collective-permute-start | bytes 196616 | tf_op jit(solution)/shard_map/ppermute | solution.py:76
  20.6 6.1 %collective-permute-start.10 = (bf16[4,4,16,128]{3,2,1,0:T(8,128)(2,1)S(1)}, bf16[4,4,16,128]{3,2,1,0:T(8,128)(2,1)S(1)}, u32[]{:S(2)}, u32[]{:S(2)}) collective-permute-start(bf16[4,4,16,128]{3,2,1,0:T(8,128)(2,1)S(1)} %bitcast.101), channel_id=1, source_target_pairs={{0,4},{1,5},{2,6},{3,7},{4,0},{5,1},{6,2},{7,3},{8,12},{9,13},{10,... | collective-permute-start | bytes 196616 | tf_op jit(solution)/shard_map/ppermute | solution.py:76
  26.7 13.3 %collective-permute-start.11 = (bf16[8,4,16,128]{3,2,1,0:T(8,128)(2,1)S(1)}, bf16[8,4,16,128]{3,2,1,0:T(8,128)(2,1)S(1)}, u32[]{:S(2)}, u32[]{:S(2)}) collective-permute-start(bf16[8,4,16,128]{3,2,1,0:T(8,128)(2,1)S(1)} %bitcast.88), channel_id=1, source_target_pairs={{0,2},{1,3},{2,0},{3,1},{4,6},{5,7},{6,4},{7,5},{8,10},{9,11},{10,... | collective-permute-start | bytes 393224 | tf_op jit(solution)/shard_map/ppermute | solution.py:76
  38.7 16.5 %copy-start = (f32[128,16,128]{2,1,0:T(8,128)S(1)}, f32[128,16,128]{2,1,0:T(8,128)}, u32[]{:S(2)}) copy-start(f32[128,16,128]{2,1,0:T(8,128)} %shard_map.46) | copy-start | bytes 3145732
  39.9 15.4 %collective-permute-start.3 = (f32[16,4,16,128]{3,2,1,0:T(8,128)S(1)}, f32[16,4,16,128]{3,2,1,0:T(8,128)S(1)}, u32[]{:S(2)}, u32[]{:S(2)}) collective-permute-start(f32[16,4,16,128]{3,2,1,0:T(8,128)S(1)} %dynamic-slice_bitcast_fusion), channel_id=1, source_target_pairs={{0,1},{1,0},{2,3},{3,2},{4,5},{5,4},{6,7},{7,6},{8,9},{9,8},{10,11... | collective-permute-start | bytes 1572872 | tf_op jit(solution)/shard_map/ppermute | solution.py:92
  40.0 2.2 %collective-permute-start.12 = (bf16[16,4,16,128]{3,2,1,0:T(8,128)(2,1)S(1)}, bf16[16,4,16,128]{3,2,1,0:T(8,128)(2,1)S(1)}, u32[]{:S(2)}, u32[]{:S(2)}) collective-permute-start(bf16[16,4,16,128]{3,2,1,0:T(8,128)(2,1)S(1)} %bitcast.81), channel_id=1, source_target_pairs={{0,1},{1,0},{2,3},{3,2},{4,5},{5,4},{6,7},{7,6},{8,9},{9,8},{10,11... | collective-permute-start | bytes 786440 | tf_op jit(solution)/shard_map/ppermute | solution.py:76
  54.6 5.6 %collective-permute-start.13 = (f32[4,4,16,128]{3,2,1,0:T(8,128)S(1)}, f32[4,4,16,128]{3,2,1,0:T(8,128)S(1)}, u32[]{:S(2)}, u32[]{:S(2)}) collective-permute-start(f32[4,4,16,128]{3,2,1,0:T(8,128)S(1)} %dynamic-slice_bitcast_fusion.2), channel_id=1, source_target_pairs={{0,32},{32,0},{64,96},{96,64},{128,160},{160,128},{192,224},{224,1... | collective-permute-start | bytes 393224 | tf_op jit(solution)/shard_map/ppermute | solution.py:92
  55.3 8.2 %collective-permute-start.4 = (f32[8,4,16,128]{3,2,1,0:T(8,128)S(1)}, f32[8,4,16,128]{3,2,1,0:T(8,128)S(1)}, u32[]{:S(2)}, u32[]{:S(2)}) collective-permute-start(f32[8,4,16,128]{3,2,1,0:T(8,128)S(1)} %dynamic-slice_bitcast_fusion.1), channel_id=1, source_target_pairs={{0,2},{1,3},{2,0},{3,1},{4,6},{5,7},{6,4},{7,5},{8,10},{9,11},{10,... | collective-permute-start | bytes 786440 | tf_op jit(solution)/shard_map/ppermute | solution.py:92
  61.1 5.7 %collective-permute-start.14 = (f32[2,4,16,128]{3,2,1,0:T(8,128)S(1)}, f32[2,4,16,128]{3,2,1,0:T(8,128)S(1)}, u32[]{:S(2)}, u32[]{:S(2)}) collective-permute-start(f32[2,4,16,128]{3,2,1,0:T(8,128)S(1)} %dynamic-slice_bitcast_fusion.4), channel_id=1, source_target_pairs={{0,64},{32,96},{64,0},{96,32},{128,192},{160,224},{192,128},{224,1... | collective-permute-start | bytes 196616 | tf_op jit(solution)/shard_map/ppermute | solution.py:92
  63.6 8.7 %collective-permute-start.5 = (f32[4,4,16,128]{3,2,1,0:T(8,128)S(1)}, f32[4,4,16,128]{3,2,1,0:T(8,128)S(1)}, u32[]{:S(2)}, u32[]{:S(2)}) collective-permute-start(f32[4,4,16,128]{3,2,1,0:T(8,128)S(1)} %dynamic-slice_bitcast_fusion.3), channel_id=1, source_target_pairs={{0,4},{1,5},{2,6},{3,7},{4,0},{5,1},{6,2},{7,3},{8,12},{9,13},{10,... | collective-permute-start | bytes 393224 | tf_op jit(solution)/shard_map/ppermute | solution.py:92
  72.3 8.3 %collective-permute-start.6 = (f32[2,4,16,128]{3,2,1,0:T(8,128)S(1)}, f32[2,4,16,128]{3,2,1,0:T(8,128)S(1)}, u32[]{:S(2)}, u32[]{:S(2)}) collective-permute-start(f32[2,4,16,128]{3,2,1,0:T(8,128)S(1)} %dynamic-slice_bitcast_fusion.5), channel_id=1, source_target_pairs={{0,8},{1,9},{2,10},{3,11},{4,12},{5,13},{6,14},{7,15},{8,0},{9,1},... | collective-permute-start | bytes 196616 | tf_op jit(solution)/shard_map/ppermute | solution.py:92
  78.0 5.4 %collective-permute-start.15 = (f32[1,4,16,128]{3,2,1,0:T(8,128)S(1)}, f32[1,4,16,128]{3,2,1,0:T(8,128)S(1)}, u32[]{:S(2)}, u32[]{:S(2)}) collective-permute-start(f32[1,4,16,128]{3,2,1,0:T(8,128)S(1)} %constant_dynamic-slice_fusion.1), channel_id=1, source_target_pairs={{0,128},{32,160},{64,192},{96,224},{128,0},{160,32},{192,64},{224,... | collective-permute-start | bytes 98312 | tf_op jit(solution)/shard_map/ppermute | solution.py:92
  80.7 5.5 %collective-permute-start.7 = (f32[1,4,16,128]{3,2,1,0:T(8,128)S(1)}, f32[1,4,16,128]{3,2,1,0:T(8,128)S(1)}, u32[]{:S(2)}, u32[]{:S(2)}) collective-permute-start(f32[1,4,16,128]{3,2,1,0:T(8,128)S(1)} %constant_dynamic-slice_fusion), channel_id=1, source_target_pairs={{0,16},{1,17},{2,18},{3,19},{4,20},{5,21},{6,22},{7,23},{8,24},{9,... | collective-permute-start | bytes 98312 | tf_op jit(solution)/shard_map/ppermute | solution.py:92

commit v3 on v2

--- a/solution.py
+++ b/solution.py
@@ -7,7 +7,7 @@
 from jax.experimental.pallas import tpu as pltpu
 from jax.sharding import PartitionSpec as P
 
-GROUP = 16
+GROUP = 64
 
 
 def _tile_kernel(rows_ref, cols_ref, count_ref, blocks_ref, vec_ref, out_ref, *, forward):

time: 87.6 us -> 80 us (0.913)
  Pallas kernels: 22.1 us -> 14.7 us
    pallas_call x2, Pallas kernels: 22.1 us -> 14.7 us  [tile_apply(): pl.pallas_call(kernel, grid_spec=grid_spec, out_shape=jax.ShapeDtypeStruc...]
  transfers between devices with their start and end apart: 16 -> 16, of which waited for: 10 -> 10; matrix products, arithmetic and copies ran while one was open for 10% -> 11% of each run, Pallas kernels for 25% -> 18%
where the time goes in v3:
time: 80 us; the launch traced here: 79.5 us
  starting transfers between devices  32 us (40%)
  waiting for transfers between devices  22.2 us (28%)
  Pallas kernels  14.7 us (18%)
  local copies, waits for them, and re-layouts  6.41 us (8%)
  other arithmetic  3.97 us (5%)
    ppermute x8, starting transfers between devices, gather_blocks(): recv = lax.ppermute(buf, axis, [(i, i ^ 1 << b) for i in range(n)])  17.7 us
    ppermute x8, waiting for transfers between devices, scatter_sum(): buf = keep + lax.ppermute(send, axis, [(i, i ^ 1 << b) for i in range(n)])  16.2 us
    pallas_call x2, Pallas kernels, tile_apply(): pl.pallas_call(kernel, grid_spec=grid_spec, out_shape=jax.ShapeDtypeStruc...  14.7 us
    ppermute x8, starting transfers between devices, scatter_sum(): buf = keep + lax.ppermute(send, axis, [(i, i ^ 1 << b) for i in range(n)])  14.3 us
    ppermute x8, waiting for transfers between devices, gather_blocks(): recv = lax.ppermute(buf, axis, [(i, i ^ 1 << b) for i in range(n)])  5.97 us
    squeeze x8, local copies, waits for them, and re-layouts, scatter_sum(): send = lax.dynamic_index_in_dim(buf, 1 - bit, 1, keepdims=False)  2.17 us
  transfers between devices with their start and end apart: 16, of which 10 were waited for; matrix products, arithmetic and copies ran while one was open for 11% of the time, Pallas kernels for 18%

profile of v3, /device:TPU:8, one launch (start us, length us, event | category | flops | bytes accessed | tf_op | source)
XLA Modules:
  0.0 79.5 jit_solution(18146071661597771081)
XLA Ops:
  0.0 0.7 reshape.303
  0.7 2.3 %collective-permute-start = (bf16[1,4,16,128]{3,1,2,0:T(4,128)(2,1)S(1)}, bf16[1,4,16,128]{3,1,2,0:T(4,128)(2,1)S(1)}, u32[]{:S(2)}, u32[]{:S(2)}) collective-permute-start(bf16[1,4,16,128]{3,1,2,0:T(4,128)(2,1)S(1)} %bitcast.94), channel_id=1, source_target_pairs={{0,128},{32,160},{64,192},{96,224},{128,0},{160,32},{192,64},{224,... | collective-permute-start | bytes 49160 | tf_op jit(solution)/shard_map/ppermute | solution.py:76
  3.0 3.0 %collective-permute-start.8 = (bf16[1,4,16,128]{3,1,2,0:T(4,128)(2,1)S(1)}, bf16[1,4,16,128]{3,1,2,0:T(4,128)(2,1)S(1)}, u32[]{:S(2)}, u32[]{:S(2)}) collective-permute-start(bf16[1,4,16,128]{3,1,2,0:T(4,128)(2,1)S(1)} %bitcast.95), channel_id=1, source_target_pairs={{0,16},{1,17},{2,18},{3,19},{4,20},{5,21},{6,22},{7,23},{8,24},{9,... | collective-permute-start | bytes 49160 | tf_op jit(solution)/shard_map/ppermute | solution.py:76
  6.0 0.7 slice_bitcast_fusion
  7.5 1.3 %broadcast_clamp_fusion = s32[1,192]{1,0:T(1,128)} fusion(s32[1,192]{1,0:T(1,128)} %param.7), kind=kLoop, calls=%fused_computation.35 | loop fusion | flops 192 | bytes 1536 | tf_op jit(solution)/shard_map/jit(clip)/min | solution.py:111
  8.7 1.2 %slice.11 = s32[1,1]{1,0:T(1,128)} slice(s32[1,129]{1,0:T(1,128)} %param.6), slice={[0:1], [128:129]} | slice | bytes 8 | tf_op jit(solution)/shard_map/slice | solution.py:112
  10.0 1.4 %collective-permute-start.1 = (bf16[2,4,16,128]{3,1,2,0:T(4,128)(2,1)S(1)}, bf16[2,4,16,128]{3,1,2,0:T(4,128)(2,1)S(1)}, u32[]{:S(2)}, u32[]{:S(2)}) collective-permute-start(bf16[2,4,16,128]{3,1,2,0:T(4,128)(2,1)S(1)} %get-tuple-element.7), channel_id=1, source_target_pairs={{0,64},{32,96},{64,0},{96,32},{128,192},{160,224},{192,128},{224,1... | collective-permute-start | bytes 98312 | tf_op jit(solution)/shard_map/ppermute | solution.py:76
  11.4 7.2 %collective-permute-start.9 = (bf16[2,4,16,128]{3,1,2,0:T(4,128)(2,1)S(1)}, bf16[2,4,16,128]{3,1,2,0:T(4,128)(2,1)S(1)}, u32[]{:S(2)}, u32[]{:S(2)}) collective-permute-start(bf16[2,4,16,128]{3,1,2,0:T(4,128)(2,1)S(1)} %get-tuple-element.8), channel_id=1, source_target_pairs={{0,8},{1,9},{2,10},{3,11},{4,12},{5,13},{6,14},{7,15},{8,0},{9,1},... | collective-permute-start | bytes 98312 | tf_op jit(solution)/shard_map/ppermute | solution.py:76
  18.8 0.7 collective-permute-start.2
  19.4 1.1 %collective-permute-done.9 = bf16[2,4,16,128]{3,1,2,0:T(4,128)(2,1)S(1)} collective-permute-done((bf16[2,4,16,128]{3,1,2,0:T(4,128)(2,1)S(1)}, bf16[2,4,16,128]{3,1,2,0:T(4,128)(2,1)S(1)}, u32[]{:S(2)}, u32[]{:S(2)}) %collective-permute-start.9) | collective-permute-done | bytes 32800 | tf_op jit(solution)/shard_map/ppermute | solution.py:76
  20.6 2.1 %collective-permute-start.10 = (bf16[4,4,16,128]{3,2,1,0:T(8,128)(2,1)S(1)}, bf16[4,4,16,128]{3,2,1,0:T(8,128)(2,1)S(1)}, u32[]{:S(2)}, u32[]{:S(2)}) collective-permute-start(bf16[4,4,16,128]{3,2,1,0:T(8,128)(2,1)S(1)} %bitcast.101), channel_id=1, source_target_pairs={{0,4},{1,5},{2,6},{3,7},{4,0},{5,1},{6,2},{7,3},{8,12},{9,13},{10,... | collective-permute-start | bytes 196616 | tf_op jit(solution)/shard_map/ppermute | solution.py:76
  23.1 0.7 copy.38
  23.8 2.8 %collective-permute-done.10 = bf16[4,4,16,128]{3,2,1,0:T(8,128)(2,1)S(1)} collective-permute-done((bf16[4,4,16,128]{3,2,1,0:T(8,128)(2,1)S(1)}, bf16[4,4,16,128]{3,2,1,0:T(8,128)(2,1)S(1)}, u32[]{:S(2)}, u32[]{:S(2)}) %collective-permute-start.10) | collective-permute-done | bytes 65568 | tf_op jit(solution)/shard_map/ppermute | solution.py:76
  27.1 8.0 %shard_map.46 = f32[128,16,128]{2,1,0:T(8,128)} custom-call(s32[192]{0:T(256)} %broadcast_minimum_fusion.rows_ref, s32[192]{0:T(256)} %bitcast.112, s32[1]{0:T(128)} %bitcast.2.count_ref, bf16[192,128,128]{2,1,0:T(8,128)(2,1)} %bitcast.74, bf16[32,16,128]{2,1,0:T(8,128)(2,1)} %bitcast.87), custom_call_target="tpu_custom_call" | custom-call | flops 100663296 | bytes 7340032 | tf_op jit(solution)/shard_map/pallas_call | solution.py:52
  35.1 1.2 %dynamic-slice_bitcast_fusion = f32[16,4,16,128]{3,2,1,0:T(8,128)S(1)} fusion(f32[16,2,4,16,128]{4,3,2,1,0:T(8,128)} %bitcast.76, s32[]{:T(128)S(6)} %select_n.215), kind=kLoop, calls=%fused_computation.2 | loop fusion | bytes 1048580 | tf_op jit(solution)/shard_map/jit(dynamic_index_in_dim)/squeeze | solution.py:91
  37.0 1.6 %collective-permute-done.12 = bf16[16,4,16,128]{3,2,1,0:T(8,128)(2,1)S(1)} collective-permute-done((bf16[16,4,16,128]{3,2,1,0:T(8,128)(2,1)S(1)}, bf16[16,4,16,128]{3,2,1,0:T(8,128)(2,1)S(1)}, u32[]{:S(2)}, u32[]{:S(2)}) %collective-permute-start.12) | collective-permute-done | bytes 262176 | tf_op jit(solution)/shard_map/ppermute | solution.py:76
  38.7 0.9 %copy.45 = bf16[16,2,4,16,128]{4,3,2,1,0:T(8,128)(2,1)} copy(bf16[16,2,4,16,128]{4,3,2,0,1:T(8,128)(2,1)S(1)} %maximum_select_fusion) | data formatting | bytes 1048576 | tf_op jit(solution)/shard_map/jit(_where)/select_n | solution.py:78
  39.6 6.7 %shard_map.47 = f32[32,16,128]{2,1,0:T(8,128)} custom-call(s32[192]{0:T(256)} %broadcast_minimum_fusion.rows_ref, s32[192]{0:T(256)} %bitcast.113, s32[1]{0:T(128)} %bitcast.2.count_ref, bf16[192,128,128]{2,1,0:T(8,128)(2,1)} %bitcast.75, bf16[128,16,128]{2,1,0:T(8,128)(2,1)} %bitcast.80), custom_call_target="tpu_custom_call" | custom-call | flops 100663296 | bytes 6553600 | tf_op jit(solution)/shard_map/pallas_call | solution.py:52
  46.2 0.9 %dynamic-slice_bitcast_fusion.2 = f32[4,4,16,128]{3,2,1,0:T(8,128)S(1)} fusion(f32[4,2,4,16,128]{4,3,2,1,0:T(8,128)} %bitcast.85, s32[]{:T(128)S(6)} %select_n.244), kind=kLoop, calls=%fused_computation.10 | loop fusion | bytes 262148 | tf_op jit(solution)/shard_map/jit(dynamic_index_in_dim)/squeeze | solution.py:91
  47.2 0.7 collective-permute-start.13
  48.0 1.8 %collective-permute-start.4 = (f32[8,4,16,128]{3,2,1,0:T(8,128)S(1)}, f32[8,4,16,128]{3,2,1,0:T(8,128)S(1)}, u32[]{:S(2)}, u32[]{:S(2)}) collective-permute-start(f32[8,4,16,128]{3,2,1,0:T(8,128)S(1)} %dynamic-slice_bitcast_fusion.1), channel_id=1, source_target_pairs={{0,2},{1,3},{2,0},{3,1},{4,6},{5,7},{6,4},{7,5},{8,10},{9,11},{10,... | collective-permute-start | bytes 786440 | tf_op jit(solution)/shard_map/ppermute | solution.py:92
  49.7 3.0 %collective-permute-done.13 = f32[4,4,16,128]{3,2,1,0:T(8,128)S(1)} collective-permute-done((f32[4,4,16,128]{3,2,1,0:T(8,128)S(1)}, f32[4,4,16,128]{3,2,1,0:T(8,128)S(1)}, u32[]{:S(2)}, u32[]{:S(2)}) %collective-permute-start.13) | collective-permute-done | bytes 131104 | tf_op jit(solution)/shard_map/ppermute | solution.py:92
  52.8 0.9 %bitcast_add_fusion.2 = f32[4,4,16,128]{3,2,1,0:T(8,128)S(1)} fusion(f32[4,4,16,128]{3,2,1,0:T(8,128)S(1)} %collective-permute-done.13, f32[4,2,4,16,128]{4,3,2,1,0:T(8,128)} %bitcast.86, s32[]{:T(128)S(6)} %select_n.243), kind=kLoop, calls=%fused_computation.8 | loop fusion | flops 32768 | bytes 393220 | tf_op jit(solution)/shard_map/add | solution.py:92
  53.7 0.8 collective-permute-start.14
  54.5 1.6 %collective-permute-done.4 = f32[8,4,16,128]{3,2,1,0:T(8,128)S(1)} collective-permute-done((f32[8,4,16,128]{3,2,1,0:T(8,128)S(1)}, f32[8,4,16,128]{3,2,1,0:T(8,128)S(1)}, u32[]{:S(2)}, u32[]{:S(2)}) %collective-permute-start.4) | collective-permute-done | bytes 262176 | tf_op jit(solution)/shard_map/ppermute | solution.py:92
  56.2 3.3 %collective-permute-start.5 = (f32[4,4,16,128]{3,2,1,0:T(8,128)S(1)}, f32[4,4,16,128]{3,2,1,0:T(8,128)S(1)}, u32[]{:S(2)}, u32[]{:S(2)}) collective-permute-start(f32[4,4,16,128]{3,2,1,0:T(8,128)S(1)} %dynamic-slice_bitcast_fusion.3), channel_id=1, source_target_pairs={{0,4},{1,5},{2,6},{3,7},{4,0},{5,1},{6,2},{7,3},{8,12},{9,13},{10,... | collective-permute-start | bytes 393224 | tf_op jit(solution)/shard_map/ppermute | solution.py:92
  59.5 5.5 %collective-permute-done.5 = f32[4,4,16,128]{3,2,1,0:T(8,128)S(1)} collective-permute-done((f32[4,4,16,128]{3,2,1,0:T(8,128)S(1)}, f32[4,4,16,128]{3,2,1,0:T(8,128)S(1)}, u32[]{:S(2)}, u32[]{:S(2)}) %collective-permute-start.5) | collective-permute-done | bytes 131104 | tf_op jit(solution)/shard_map/ppermute | solution.py:92
  64.9 5.6 %collective-permute-start.6 = (f32[2,4,16,128]{3,2,1,0:T(8,128)S(1)}, f32[2,4,16,128]{3,2,1,0:T(8,128)S(1)}, u32[]{:S(2)}, u32[]{:S(2)}) collective-permute-start(f32[2,4,16,128]{3,2,1,0:T(8,128)S(1)} %dynamic-slice_bitcast_fusion.5), channel_id=1, source_target_pairs={{0,8},{1,9},{2,10},{3,11},{4,12},{5,13},{6,14},{7,15},{8,0},{9,1},... | collective-permute-start | bytes 196616 | tf_op jit(solution)/shard_map/ppermute | solution.py:92
  70.6 2.7 %collective-permute-done.6 = f32[2,4,16,128]{3,2,1,0:T(8,128)S(1)} collective-permute-done((f32[2,4,16,128]{3,2,1,0:T(8,128)S(1)}, f32[2,4,16,128]{3,2,1,0:T(8,128)S(1)}, u32[]{:S(2)}, u32[]{:S(2)}) %collective-permute-start.6) | collective-permute-done | bytes 65568 | tf_op jit(solution)/shard_map/ppermute | solution.py:92
  73.3 2.1 %collective-permute-start.7 = (f32[1,4,16,128]{3,2,1,0:T(8,128)S(1)}, f32[1,4,16,128]{3,2,1,0:T(8,128)S(1)}, u32[]{:S(2)}, u32[]{:S(2)}) collective-permute-start(f32[1,4,16,128]{3,2,1,0:T(8,128)S(1)} %constant_dynamic-slice_fusion), channel_id=1, source_target_pairs={{0,16},{1,17},{2,18},{3,19},{4,20},{5,21},{6,22},{7,23},{8,24},{9,... | collective-permute-start | bytes 98312 | tf_op jit(solution)/shard_map/ppermute | solution.py:92
  76.0 2.9 %collective-permute-done.7 = f32[1,4,16,128]{3,2,1,0:T(8,128)S(1)} collective-permute-done((f32[1,4,16,128]{3,2,1,0:T(8,128)S(1)}, f32[1,4,16,128]{3,2,1,0:T(8,128)S(1)}, u32[]{:S(2)}, u32[]{:S(2)}) %collective-permute-start.7) | collective-permute-done | bytes 32800 | tf_op jit(solution)/shard_map/ppermute | solution.py:92
  78.8 0.6 copy_bitcast_fusion
  (39 shorter events, 3.4 us)
Async XLA Ops:
  0.7 9.2 %collective-permute-start = (bf16[1,4,16,128]{3,1,2,0:T(4,128)(2,1)S(1)}, bf16[1,4,16,128]{3,1,2,0:T(4,128)(2,1)S(1)}, u32[]{:S(2)}, u32[]{:S(2)}) collective-permute-start(bf16[1,4,16,128]{3,1,2,0:T(4,128)(2,1)S(1)} %bitcast.94), channel_id=1, source_target_pairs={{0,128},{32,160},{64,192},{96,224},{128,0},{160,32},{192,64},{224,... | collective-permute-start | bytes 49160 | tf_op jit(solution)/shard_map/ppermute | solution.py:76
  3.0 6.9 %collective-permute-start.8 = (bf16[1,4,16,128]{3,1,2,0:T(4,128)(2,1)S(1)}, bf16[1,4,16,128]{3,1,2,0:T(4,128)(2,1)S(1)}, u32[]{:S(2)}, u32[]{:S(2)}) collective-permute-start(bf16[1,4,16,128]{3,1,2,0:T(4,128)(2,1)S(1)} %bitcast.95), channel_id=1, source_target_pairs={{0,16},{1,17},{2,18},{3,19},{4,20},{5,21},{6,22},{7,23},{8,24},{9,... | collective-permute-start | bytes 49160 | tf_op jit(solution)/shard_map/ppermute | solution.py:76
  10.0 8.7 %collective-permute-start.1 = (bf16[2,4,16,128]{3,1,2,0:T(4,128)(2,1)S(1)}, bf16[2,4,16,128]{3,1,2,0:T(4,128)(2,1)S(1)}, u32[]{:S(2)}, u32[]{:S(2)}) collective-permute-start(bf16[2,4,16,128]{3,1,2,0:T(4,128)(2,1)S(1)} %get-tuple-element.7), channel_id=1, source_target_pairs={{0,64},{32,96},{64,0},{96,32},{128,192},{160,224},{192,128},{224,1... | collective-permute-start | bytes 98312 | tf_op jit(solution)/shard_map/ppermute | solution.py:76
  11.4 9.1 %collective-permute-start.9 = (bf16[2,4,16,128]{3,1,2,0:T(4,128)(2,1)S(1)}, bf16[2,4,16,128]{3,1,2,0:T(4,128)(2,1)S(1)}, u32[]{:S(2)}, u32[]{:S(2)}) collective-permute-start(bf16[2,4,16,128]{3,1,2,0:T(4,128)(2,1)S(1)} %get-tuple-element.8), channel_id=1, source_target_pairs={{0,8},{1,9},{2,10},{3,11},{4,12},{5,13},{6,14},{7,15},{8,0},{9,1},... | collective-permute-start | bytes 98312 | tf_op jit(solution)/shard_map/ppermute | solution.py:76
  18.8 4.4 %collective-permute-start.2 = (bf16[4,4,16,128]{3,2,1,0:T(8,128)(2,1)S(1)}, bf16[4,4,16,128]{3,2,1,0:T(8,128)(2,1)S(1)}, u32[]{:S(2)}, u32[]{:S(2)}) collective-permute-start(bf16[4,4,16,128]{3,2,1,0:T(8,128)(2,1)S(1)} %bitcast.99), channel_id=1, source_target_pairs={{0,32},{32,0},{64,96},{96,64},{128,160},{160,128},{192,224},{224,1... | collective-permute-start | bytes 196616 | tf_op jit(solution)/shard_map/ppermute | solution.py:76
  20.6 6.1 %collective-permute-start.10 = (bf16[4,4,16,128]{3,2,1,0:T(8,128)(2,1)S(1)}, bf16[4,4,16,128]{3,2,1,0:T(8,128)(2,1)S(1)}, u32[]{:S(2)}, u32[]{:S(2)}) collective-permute-start(bf16[4,4,16,128]{3,2,1,0:T(8,128)(2,1)S(1)} %bitcast.101), channel_id=1, source_target_pairs={{0,4},{1,5},{2,6},{3,7},{4,0},{5,1},{6,2},{7,3},{8,12},{9,13},{10,... | collective-permute-start | bytes 196616 | tf_op jit(solution)/shard_map/ppermute | solution.py:76
  26.7 9.7 %collective-permute-start.11 = (bf16[8,4,16,128]{3,2,1,0:T(8,128)(2,1)S(1)}, bf16[8,4,16,128]{3,2,1,0:T(8,128)(2,1)S(1)}, u32[]{:S(2)}, u32[]{:S(2)}) collective-permute-start(bf16[8,4,16,128]{3,2,1,0:T(8,128)(2,1)S(1)} %bitcast.88), channel_id=1, source_target_pairs={{0,2},{1,3},{2,0},{3,1},{4,6},{5,7},{6,4},{7,5},{8,10},{9,11},{10,... | collective-permute-start | bytes 393224 | tf_op jit(solution)/shard_map/ppermute | solution.py:76
  35.1 12.8 %copy-start = (f32[128,16,128]{2,1,0:T(8,128)S(1)}, f32[128,16,128]{2,1,0:T(8,128)}, u32[]{:S(2)}) copy-start(f32[128,16,128]{2,1,0:T(8,128)} %shard_map.46) | copy-start | bytes 3145732
  36.3 11.6 %collective-permute-start.3 = (f32[16,4,16,128]{3,2,1,0:T(8,128)S(1)}, f32[16,4,16,128]{3,2,1,0:T(8,128)S(1)}, u32[]{:S(2)}, u32[]{:S(2)}) collective-permute-start(f32[16,4,16,128]{3,2,1,0:T(8,128)S(1)} %dynamic-slice_bitcast_fusion), channel_id=1, source_target_pairs={{0,1},{1,0},{2,3},{3,2},{4,5},{5,4},{6,7},{7,6},{8,9},{9,8},{10,11... | collective-permute-start | bytes 1572872 | tf_op jit(solution)/shard_map/ppermute | solution.py:92
  36.4 2.2 %collective-permute-start.12 = (bf16[16,4,16,128]{3,2,1,0:T(8,128)(2,1)S(1)}, bf16[16,4,16,128]{3,2,1,0:T(8,128)(2,1)S(1)}, u32[]{:S(2)}, u32[]{:S(2)}) collective-permute-start(bf16[16,4,16,128]{3,2,1,0:T(8,128)(2,1)S(1)} %bitcast.81), channel_id=1, source_target_pairs={{0,1},{1,0},{2,3},{3,2},{4,5},{5,4},{6,7},{7,6},{8,9},{9,8},{10,11... | collective-permute-start | bytes 786440 | tf_op jit(solution)/shard_map/ppermute | solution.py:76
  47.2 5.6 %collective-permute-start.13 = (f32[4,4,16,128]{3,2,1,0:T(8,128)S(1)}, f32[4,4,16,128]{3,2,1,0:T(8,128)S(1)}, u32[]{:S(2)}, u32[]{:S(2)}) collective-permute-start(f32[4,4,16,128]{3,2,1,0:T(8,128)S(1)} %dynamic-slice_bitcast_fusion.2), channel_id=1, source_target_pairs={{0,32},{32,0},{64,96},{96,64},{128,160},{160,128},{192,224},{224,1... | collective-permute-start | bytes 393224 | tf_op jit(solution)/shard_map/ppermute | solution.py:92
  48.0 8.2 %collective-permute-start.4 = (f32[8,4,16,128]{3,2,1,0:T(8,128)S(1)}, f32[8,4,16,128]{3,2,1,0:T(8,128)S(1)}, u32[]{:S(2)}, u32[]{:S(2)}) collective-permute-start(f32[8,4,16,128]{3,2,1,0:T(8,128)S(1)} %dynamic-slice_bitcast_fusion.1), channel_id=1, source_target_pairs={{0,2},{1,3},{2,0},{3,1},{4,6},{5,7},{6,4},{7,5},{8,10},{9,11},{10,... | collective-permute-start | bytes 786440 | tf_op jit(solution)/shard_map/ppermute | solution.py:92
  53.7 5.7 %collective-permute-start.14 = (f32[2,4,16,128]{3,2,1,0:T(8,128)S(1)}, f32[2,4,16,128]{3,2,1,0:T(8,128)S(1)}, u32[]{:S(2)}, u32[]{:S(2)}) collective-permute-start(f32[2,4,16,128]{3,2,1,0:T(8,128)S(1)} %dynamic-slice_bitcast_fusion.4), channel_id=1, source_target_pairs={{0,64},{32,96},{64,0},{96,32},{128,192},{160,224},{192,128},{224,1... | collective-permute-start | bytes 196616 | tf_op jit(solution)/shard_map/ppermute | solution.py:92
  56.2 8.7 %collective-permute-start.5 = (f32[4,4,16,128]{3,2,1,0:T(8,128)S(1)}, f32[4,4,16,128]{3,2,1,0:T(8,128)S(1)}, u32[]{:S(2)}, u32[]{:S(2)}) collective-permute-start(f32[4,4,16,128]{3,2,1,0:T(8,128)S(1)} %dynamic-slice_bitcast_fusion.3), channel_id=1, source_target_pairs={{0,4},{1,5},{2,6},{3,7},{4,0},{5,1},{6,2},{7,3},{8,12},{9,13},{10,... | collective-permute-start | bytes 393224 | tf_op jit(solution)/shard_map/ppermute | solution.py:92
  64.9 8.4 %collective-permute-start.6 = (f32[2,4,16,128]{3,2,1,0:T(8,128)S(1)}, f32[2,4,16,128]{3,2,1,0:T(8,128)S(1)}, u32[]{:S(2)}, u32[]{:S(2)}) collective-permute-start(f32[2,4,16,128]{3,2,1,0:T(8,128)S(1)} %dynamic-slice_bitcast_fusion.5), channel_id=1, source_target_pairs={{0,8},{1,9},{2,10},{3,11},{4,12},{5,13},{6,14},{7,15},{8,0},{9,1},... | collective-permute-start | bytes 196616 | tf_op jit(solution)/shard_map/ppermute | solution.py:92
  70.6 5.4 %collective-permute-start.15 = (f32[1,4,16,128]{3,2,1,0:T(8,128)S(1)}, f32[1,4,16,128]{3,2,1,0:T(8,128)S(1)}, u32[]{:S(2)}, u32[]{:S(2)}) collective-permute-start(f32[1,4,16,128]{3,2,1,0:T(8,128)S(1)} %constant_dynamic-slice_fusion.1), channel_id=1, source_target_pairs={{0,128},{32,160},{64,192},{96,224},{128,0},{160,32},{192,64},{224,... | collective-permute-start | bytes 98312 | tf_op jit(solution)/shard_map/ppermute | solution.py:92
  73.3 5.5 %collective-permute-start.7 = (f32[1,4,16,128]{3,2,1,0:T(8,128)S(1)}, f32[1,4,16,128]{3,2,1,0:T(8,128)S(1)}, u32[]{:S(2)}, u32[]{:S(2)}) collective-permute-start(f32[1,4,16,128]{3,2,1,0:T(8,128)S(1)} %constant_dynamic-slice_fusion), channel_id=1, source_target_pairs={{0,16},{1,17},{2,18},{3,19},{4,20},{5,21},{6,22},{7,23},{8,24},{9,... | collective-permute-start | bytes 98312 | tf_op jit(solution)/shard_map/ppermute | solution.py:92

commit v4 on v3

--- a/solution.py
+++ b/solution.py
@@ -7,7 +7,7 @@
 from jax.experimental.pallas import tpu as pltpu
 from jax.sharding import PartitionSpec as P
 
-GROUP = 64
+GROUP = 96
 
 
 def _tile_kernel(rows_ref, cols_ref, count_ref, blocks_ref, vec_ref, out_ref, *, forward):
@@ -17,7 +17,7 @@
     def _():
         out_ref[...] = jnp.zeros_like(out_ref)
 
-    count = count_ref[0]
+    count = count_ref[count_ref.shape[0] - 1]
     parts = []
     for t in range(GROUP):
         s = g * GROUP + t
@@ -106,10 +106,10 @@
     tile_cols = grid_rows * seg_blocks
 
     slot_ids = jnp.arange(slots, dtype=jnp.int32)
-    slot_rows = jnp.sum((slot_ids[:, None] >= pointers[None, 1:]).astype(jnp.int32), axis=1)
-    slot_rows = jnp.minimum(slot_rows, tile_rows - 1).astype(jnp.int32)
-    columns = jnp.clip(columns, 0, tile_cols - 1).astype(jnp.int32)
-    count = pointers[-1:].astype(jnp.int32)
+    slot_rows = jnp.sum((slot_ids[:, None] >= pointers[None, :]).astype(jnp.int32), axis=1)
+    slot_rows = jnp.minimum(slot_rows - 1, tile_rows - 1).astype(jnp.int32)
+    columns = columns.astype(jnp.int32)
+    count = pointers.astype(jnp.int32)
 
     own = vectors.reshape(count_vectors, seg_blocks, edge).transpose(1, 0, 2)
     col_side = gather_blocks(own, "row")

time: 80 us -> 77.1 us (0.964)
  starting transfers between devices: 32 us -> 34.8 us
  Pallas kernels: 14.7 us -> 12.6 us
  local copies, waits for them, and re-layouts: 6.41 us -> 4.49 us
    pallas_call x2, Pallas kernels: 14.7 us -> 12.6 us  [tile_apply(): pl.pallas_call(kernel, grid_spec=grid_spec, out_shape=jax.ShapeDtypeStruc...]
    ppermute x8, starting transfers between devices: 17.7 us -> 19.7 us  [gather_blocks(): recv = lax.ppermute(buf, axis, [(i, i ^ 1 << b) for i in range(n)])]
    min x2 -> x1, other arithmetic: 1.83 us -> 0.57 us  [body(): slot_rows = jnp.minimum(slot_rows - 1, tile_rows - 1).astype(jnp.int32)]
    slice x1 -> x0, local copies, waits for them, and re-layouts: 1.17 us -> none  [body(): count = pointers[-1:].astype(jnp.int32)]
    ppermute x8, waiting for transfers between devices: 5.97 us -> 5.13 us  [gather_blocks(): recv = lax.ppermute(buf, axis, [(i, i ^ 1 << b) for i in range(n)])]
  transfers between devices with their start and end apart: 16 -> 16, of which waited for: 10 -> 11; matrix products, arithmetic and copies ran while one was open for 11% -> 8% of each run, Pallas kernels for 18% -> 16%
where the time goes in v4:
time: 77.1 us; the launch traced here: 76.9 us
  starting transfers between devices  34.8 us (45%)
  waiting for transfers between devices  21.5 us (28%)
  Pallas kernels  12.6 us (16%)
  local copies, waits for them, and re-layouts  4.49 us (6%)
  other arithmetic  3.37 us (4%)
    ppermute x8, starting transfers between devices, gather_blocks(): recv = lax.ppermute(buf, axis, [(i, i ^ 1 << b) for i in range(n)])  19.7 us
    ppermute x8, waiting for transfers between devices, scatter_sum(): buf = keep + lax.ppermute(send, axis, [(i, i ^ 1 << b) for i in range(n)])  16.3 us
    ppermute x8, starting transfers between devices, scatter_sum(): buf = keep + lax.ppermute(send, axis, [(i, i ^ 1 << b) for i in range(n)])  15.1 us
    pallas_call x2, Pallas kernels, tile_apply(): pl.pallas_call(kernel, grid_spec=grid_spec, out_shape=jax.ShapeDtypeStruc...  12.6 us
    ppermute x8, waiting for transfers between devices, gather_blocks(): recv = lax.ppermute(buf, axis, [(i, i ^ 1 << b) for i in range(n)])  5.13 us
    squeeze x8, local copies, waits for them, and re-layouts, scatter_sum(): send = lax.dynamic_index_in_dim(buf, 1 - bit, 1, keepdims=False)  2.17 us
    select_n x6, local copies, waits for them, and re-layouts, gather_blocks(): buf = jnp.where(low, jnp.stack([buf, recv], 1), jnp.stack([recv, buf], 1))  1.59 us
  transfers between devices with their start and end apart: 16, of which 11 were waited for; matrix products, arithmetic and copies ran while one was open for 8% of the time, Pallas kernels for 16%

profile of v4, /device:TPU:8, one launch (start us, length us, event | category | flops | bytes accessed | tf_op | source)
XLA Modules:
  0.0 76.9 jit_solution(2863909383764907408)
XLA Ops:
  0.0 0.7 reshape.297
  0.7 2.3 %collective-permute-start = (bf16[1,4,16,128]{3,1,2,0:T(4,128)(2,1)S(1)}, bf16[1,4,16,128]{3,1,2,0:T(4,128)(2,1)S(1)}, u32[]{:S(2)}, u32[]{:S(2)}) collective-permute-start(bf16[1,4,16,128]{3,1,2,0:T(4,128)(2,1)S(1)} %bitcast.92), channel_id=1, source_target_pairs={{0,128},{32,160},{64,192},{96,224},{128,0},{160,32},{192,64},{224,... | collective-permute-start | bytes 49160 | tf_op jit(solution)/shard_map/ppermute | solution.py:76
  3.0 3.0 %collective-permute-start.8 = (bf16[1,4,16,128]{3,1,2,0:T(4,128)(2,1)S(1)}, bf16[1,4,16,128]{3,1,2,0:T(4,128)(2,1)S(1)}, u32[]{:S(2)}, u32[]{:S(2)}) collective-permute-start(bf16[1,4,16,128]{3,1,2,0:T(4,128)(2,1)S(1)} %bitcast.93), channel_id=1, source_target_pairs={{0,16},{1,17},{2,18},{3,19},{4,20},{5,21},{6,22},{7,23},{8,24},{9,... | collective-permute-start | bytes 49160 | tf_op jit(solution)/shard_map/ppermute | solution.py:76
  6.0 0.8 %convert_reduce_fusion = s32[192]{0:T(256)S(1)} fusion(s32[129]{0:T(256)} %bitcast.110), kind=kLoop, calls=%fused_computation.6 | loop fusion | flops 74112 | bytes 1284 | tf_op jit(solution)/shard_map/reduce_sum | solution.py:109
  7.4 0.9 %collective-permute-done.8 = bf16[1,4,16,128]{3,1,2,0:T(4,128)(2,1)S(1)} collective-permute-done((bf16[1,4,16,128]{3,1,2,0:T(4,128)(2,1)S(1)}, bf16[1,4,16,128]{3,1,2,0:T(4,128)(2,1)S(1)}, u32[]{:S(2)}, u32[]{:S(2)}) %collective-permute-start.8) | collective-permute-done | bytes 16416 | tf_op jit(solution)/shard_map/ppermute | solution.py:76
  8.3 1.4 %collective-permute-start.1 = (bf16[2,4,16,128]{3,1,2,0:T(4,128)(2,1)S(1)}, bf16[2,4,16,128]{3,1,2,0:T(4,128)(2,1)S(1)}, u32[]{:S(2)}, u32[]{:S(2)}) collective-permute-start(bf16[2,4,16,128]{3,1,2,0:T(4,128)(2,1)S(1)} %get-tuple-element.7), channel_id=1, source_target_pairs={{0,64},{32,96},{64,0},{96,32},{128,192},{160,224},{192,128},{224,1... | collective-permute-start | bytes 98312 | tf_op jit(solution)/shard_map/ppermute | solution.py:76
  9.8 7.2 %collective-permute-start.9 = (bf16[2,4,16,128]{3,1,2,0:T(4,128)(2,1)S(1)}, bf16[2,4,16,128]{3,1,2,0:T(4,128)(2,1)S(1)}, u32[]{:S(2)}, u32[]{:S(2)}) collective-permute-start(bf16[2,4,16,128]{3,1,2,0:T(4,128)(2,1)S(1)} %get-tuple-element.8), channel_id=1, source_target_pairs={{0,8},{1,9},{2,10},{3,11},{4,12},{5,13},{6,14},{7,15},{8,0},{9,1},... | collective-permute-start | bytes 98312 | tf_op jit(solution)/shard_map/ppermute | solution.py:76
  17.1 1.6 %collective-permute-start.2 = (bf16[4,4,16,128]{3,2,1,0:T(8,128)(2,1)S(1)}, bf16[4,4,16,128]{3,2,1,0:T(8,128)(2,1)S(1)}, u32[]{:S(2)}, u32[]{:S(2)}) collective-permute-start(bf16[4,4,16,128]{3,2,1,0:T(8,128)(2,1)S(1)} %bitcast.97), channel_id=1, source_target_pairs={{0,32},{32,0},{64,96},{96,64},{128,160},{160,128},{192,224},{224,1... | collective-permute-start | bytes 196616 | tf_op jit(solution)/shard_map/ppermute | solution.py:76
  18.9 2.1 %collective-permute-start.10 = (bf16[4,4,16,128]{3,2,1,0:T(8,128)(2,1)S(1)}, bf16[4,4,16,128]{3,2,1,0:T(8,128)(2,1)S(1)}, u32[]{:S(2)}, u32[]{:S(2)}) collective-permute-start(bf16[4,4,16,128]{3,2,1,0:T(8,128)(2,1)S(1)} %bitcast.99), channel_id=1, source_target_pairs={{0,4},{1,5},{2,6},{3,7},{4,0},{5,1},{6,2},{7,3},{8,12},{9,13},{10,... | collective-permute-start | bytes 196616 | tf_op jit(solution)/shard_map/ppermute | solution.py:76
  21.5 0.7 copy.38
  22.1 2.0 %collective-permute-done.10 = bf16[4,4,16,128]{3,2,1,0:T(8,128)(2,1)S(1)} collective-permute-done((bf16[4,4,16,128]{3,2,1,0:T(8,128)(2,1)S(1)}, bf16[4,4,16,128]{3,2,1,0:T(8,128)(2,1)S(1)}, u32[]{:S(2)}, u32[]{:S(2)}) %collective-permute-start.10) | collective-permute-done | bytes 65568 | tf_op jit(solution)/shard_map/ppermute | solution.py:76
  24.2 1.5 %collective-permute-start.11 = (bf16[8,4,16,128]{3,2,1,0:T(8,128)(2,1)S(1)}, bf16[8,4,16,128]{3,2,1,0:T(8,128)(2,1)S(1)}, u32[]{:S(2)}, u32[]{:S(2)}) collective-permute-start(bf16[8,4,16,128]{3,2,1,0:T(8,128)(2,1)S(1)} %bitcast.86), channel_id=1, source_target_pairs={{0,2},{1,3},{2,0},{3,1},{4,6},{5,7},{6,4},{7,5},{8,10},{9,11},{10,... | collective-permute-start | bytes 393224 | tf_op jit(solution)/shard_map/ppermute | solution.py:76
  25.7 7.2 %shard_map.46 = f32[128,16,128]{2,1,0:T(8,128)} custom-call(s32[192]{0:T(256)} %add_minimum_fusion.rows_ref, s32[192]{0:T(256)} %bitcast.113, s32[129]{0:T(256)} %bitcast.111, bf16[192,128,128]{2,1,0:T(8,128)(2,1)} %bitcast.72, bf16[32,16,128]{2,1,0:T(8,128)(2,1)} %bitcast.85), custom_call_target="tpu_custom_call" | custom-call | flops 100663296 | bytes 7340032 | tf_op jit(solution)/shard_map/pallas_call | solution.py:52
  33.0 1.2 %dynamic-slice_bitcast_fusion = f32[16,4,16,128]{3,2,1,0:T(8,128)S(1)} fusion(f32[16,2,4,16,128]{4,3,2,1,0:T(8,128)} %bitcast.74, s32[]{:T(128)S(6)} %select_n.215), kind=kLoop, calls=%fused_computation.2 | loop fusion | bytes 1048580 | tf_op jit(solution)/shard_map/jit(dynamic_index_in_dim)/squeeze | solution.py:91
  34.3 0.6 collective-permute-start.12
  34.9 1.6 %collective-permute-done.12 = bf16[16,4,16,128]{3,2,1,0:T(8,128)(2,1)S(1)} collective-permute-done((bf16[16,4,16,128]{3,2,1,0:T(8,128)(2,1)S(1)}, bf16[16,4,16,128]{3,2,1,0:T(8,128)(2,1)S(1)}, u32[]{:S(2)}, u32[]{:S(2)}) %collective-permute-start.12) | collective-permute-done | bytes 262176 | tf_op jit(solution)/shard_map/ppermute | solution.py:76
  36.6 0.9 %copy.45 = bf16[16,2,4,16,128]{4,3,2,1,0:T(8,128)(2,1)} copy(bf16[16,2,4,16,128]{4,3,2,0,1:T(8,128)(2,1)S(1)} %maximum_select_fusion) | data formatting | bytes 1048576 | tf_op jit(solution)/shard_map/jit(_where)/select_n | solution.py:78
  37.5 5.4 %shard_map.47 = f32[32,16,128]{2,1,0:T(8,128)} custom-call(s32[192]{0:T(256)} %add_minimum_fusion.rows_ref, s32[192]{0:T(256)} %bitcast.114, s32[129]{0:T(256)} %bitcast.112, bf16[192,128,128]{2,1,0:T(8,128)(2,1)} %bitcast.73, bf16[128,16,128]{2,1,0:T(8,128)(2,1)} %bitcast.78), custom_call_target="tpu_custom_call" | custom-call | flops 100663296 | bytes 6553600 | tf_op jit(solution)/shard_map/pallas_call | solution.py:52
  42.9 0.9 %dynamic-slice_bitcast_fusion.2 = f32[4,4,16,128]{3,2,1,0:T(8,128)S(1)} fusion(f32[4,2,4,16,128]{4,3,2,1,0:T(8,128)} %bitcast.79, s32[]{:T(128)S(6)} %select_n.244), kind=kLoop, calls=%fused_computation.12 | loop fusion | bytes 262148 | tf_op jit(solution)/shard_map/jit(dynamic_index_in_dim)/squeeze | solution.py:91
  43.8 1.6 %collective-permute-start.13 = (f32[4,4,16,128]{3,2,1,0:T(8,128)S(1)}, f32[4,4,16,128]{3,2,1,0:T(8,128)S(1)}, u32[]{:S(2)}, u32[]{:S(2)}) collective-permute-start(f32[4,4,16,128]{3,2,1,0:T(8,128)S(1)} %dynamic-slice_bitcast_fusion.2), channel_id=1, source_target_pairs={{0,32},{32,0},{64,96},{96,64},{128,160},{160,128},{192,224},{224,1... | collective-permute-start | bytes 393224 | tf_op jit(solution)/shard_map/ppermute | solution.py:92
  45.5 0.6 collective-permute-start.4
  46.2 3.3 %collective-permute-done.13 = f32[4,4,16,128]{3,2,1,0:T(8,128)S(1)} collective-permute-done((f32[4,4,16,128]{3,2,1,0:T(8,128)S(1)}, f32[4,4,16,128]{3,2,1,0:T(8,128)S(1)}, u32[]{:S(2)}, u32[]{:S(2)}) %collective-permute-start.13) | collective-permute-done | bytes 131104 | tf_op jit(solution)/shard_map/ppermute | solution.py:92
  49.4 0.9 %bitcast_add_fusion.2 = f32[4,4,16,128]{3,2,1,0:T(8,128)S(1)} fusion(f32[4,4,16,128]{3,2,1,0:T(8,128)S(1)} %collective-permute-done.13, f32[4,2,4,16,128]{4,3,2,1,0:T(8,128)} %bitcast.80, s32[]{:T(128)S(6)} %select_n.243), kind=kLoop, calls=%fused_computation.10 | loop fusion | flops 32768 | bytes 393220 | tf_op jit(solution)/shard_map/add | solution.py:92
  50.4 0.8 collective-permute-start.14
  51.1 2.6 %collective-permute-done.4 = f32[8,4,16,128]{3,2,1,0:T(8,128)S(1)} collective-permute-done((f32[8,4,16,128]{3,2,1,0:T(8,128)S(1)}, f32[8,4,16,128]{3,2,1,0:T(8,128)S(1)}, u32[]{:S(2)}, u32[]{:S(2)}) %collective-permute-start.4) | collective-permute-done | bytes 262176 | tf_op jit(solution)/shard_map/ppermute | solution.py:92
  53.8 3.3 %collective-permute-start.5 = (f32[4,4,16,128]{3,2,1,0:T(8,128)S(1)}, f32[4,4,16,128]{3,2,1,0:T(8,128)S(1)}, u32[]{:S(2)}, u32[]{:S(2)}) collective-permute-start(f32[4,4,16,128]{3,2,1,0:T(8,128)S(1)} %dynamic-slice_bitcast_fusion.3), channel_id=1, source_target_pairs={{0,4},{1,5},{2,6},{3,7},{4,0},{5,1},{6,2},{7,3},{8,12},{9,13},{10,... | collective-permute-start | bytes 393224 | tf_op jit(solution)/shard_map/ppermute | solution.py:92
  57.0 5.4 %collective-permute-done.5 = f32[4,4,16,128]{3,2,1,0:T(8,128)S(1)} collective-permute-done((f32[4,4,16,128]{3,2,1,0:T(8,128)S(1)}, f32[4,4,16,128]{3,2,1,0:T(8,128)S(1)}, u32[]{:S(2)}, u32[]{:S(2)}) %collective-permute-start.5) | collective-permute-done | bytes 131104 | tf_op jit(solution)/shard_map/ppermute | solution.py:92
  62.5 5.9 %collective-permute-start.6 = (f32[2,4,16,128]{3,2,1,0:T(8,128)S(1)}, f32[2,4,16,128]{3,2,1,0:T(8,128)S(1)}, u32[]{:S(2)}, u32[]{:S(2)}) collective-permute-start(f32[2,4,16,128]{3,2,1,0:T(8,128)S(1)} %dynamic-slice_bitcast_fusion.5), channel_id=1, source_target_pairs={{0,8},{1,9},{2,10},{3,11},{4,12},{5,13},{6,14},{7,15},{8,0},{9,1},... | collective-permute-start | bytes 196616 | tf_op jit(solution)/shard_map/ppermute | solution.py:92
  68.4 2.4 %collective-permute-done.6 = f32[2,4,16,128]{3,2,1,0:T(8,128)S(1)} collective-permute-done((f32[2,4,16,128]{3,2,1,0:T(8,128)S(1)}, f32[2,4,16,128]{3,2,1,0:T(8,128)S(1)}, u32[]{:S(2)}, u32[]{:S(2)}) %collective-permute-start.6) | collective-permute-done | bytes 65568 | tf_op jit(solution)/shard_map/ppermute | solution.py:92
  70.8 2.8 %collective-permute-start.7 = (f32[1,4,16,128]{3,2,1,0:T(8,128)S(1)}, f32[1,4,16,128]{3,2,1,0:T(8,128)S(1)}, u32[]{:S(2)}, u32[]{:S(2)}) collective-permute-start(f32[1,4,16,128]{3,2,1,0:T(8,128)S(1)} %constant_dynamic-slice_fusion), channel_id=1, source_target_pairs={{0,16},{1,17},{2,18},{3,19},{4,20},{5,21},{6,22},{7,23},{8,24},{9,... | collective-permute-start | bytes 98312 | tf_op jit(solution)/shard_map/ppermute | solution.py:92
  73.8 2.5 %collective-permute-done.7 = f32[1,4,16,128]{3,2,1,0:T(8,128)S(1)} collective-permute-done((f32[1,4,16,128]{3,2,1,0:T(8,128)S(1)}, f32[1,4,16,128]{3,2,1,0:T(8,128)S(1)}, u32[]{:S(2)}, u32[]{:S(2)}) %collective-permute-start.7) | collective-permute-done | bytes 32800 | tf_op jit(solution)/shard_map/ppermute | solution.py:92
  76.3 0.6 copy_bitcast_fusion
  (36 shorter events, 2.1 us)
Async XLA Ops:
  0.7 6.7 %collective-permute-start = (bf16[1,4,16,128]{3,1,2,0:T(4,128)(2,1)S(1)}, bf16[1,4,16,128]{3,1,2,0:T(4,128)(2,1)S(1)}, u32[]{:S(2)}, u32[]{:S(2)}) collective-permute-start(bf16[1,4,16,128]{3,1,2,0:T(4,128)(2,1)S(1)} %bitcast.92), channel_id=1, source_target_pairs={{0,128},{32,160},{64,192},{96,224},{128,0},{160,32},{192,64},{224,... | collective-permute-start | bytes 49160 | tf_op jit(solution)/shard_map/ppermute | solution.py:76
  3.0 5.2 %collective-permute-start.8 = (bf16[1,4,16,128]{3,1,2,0:T(4,128)(2,1)S(1)}, bf16[1,4,16,128]{3,1,2,0:T(4,128)(2,1)S(1)}, u32[]{:S(2)}, u32[]{:S(2)}) collective-permute-start(bf16[1,4,16,128]{3,1,2,0:T(4,128)(2,1)S(1)} %bitcast.93), channel_id=1, source_target_pairs={{0,16},{1,17},{2,18},{3,19},{4,20},{5,21},{6,22},{7,23},{8,24},{9,... | collective-permute-start | bytes 49160 | tf_op jit(solution)/shard_map/ppermute | solution.py:76
  8.3 8.7 %collective-permute-start.1 = (bf16[2,4,16,128]{3,1,2,0:T(4,128)(2,1)S(1)}, bf16[2,4,16,128]{3,1,2,0:T(4,128)(2,1)S(1)}, u32[]{:S(2)}, u32[]{:S(2)}) collective-permute-start(bf16[2,4,16,128]{3,1,2,0:T(4,128)(2,1)S(1)} %get-tuple-element.7), channel_id=1, source_target_pairs={{0,64},{32,96},{64,0},{96,32},{128,192},{160,224},{192,128},{224,1... | collective-permute-start | bytes 98312 | tf_op jit(solution)/shard_map/ppermute | solution.py:76
  9.8 9.1 %collective-permute-start.9 = (bf16[2,4,16,128]{3,1,2,0:T(4,128)(2,1)S(1)}, bf16[2,4,16,128]{3,1,2,0:T(4,128)(2,1)S(1)}, u32[]{:S(2)}, u32[]{:S(2)}) collective-permute-start(bf16[2,4,16,128]{3,1,2,0:T(4,128)(2,1)S(1)} %get-tuple-element.8), channel_id=1, source_target_pairs={{0,8},{1,9},{2,10},{3,11},{4,12},{5,13},{6,14},{7,15},{8,0},{9,1},... | collective-permute-start | bytes 98312 | tf_op jit(solution)/shard_map/ppermute | solution.py:76
  17.1 4.4 %collective-permute-start.2 = (bf16[4,4,16,128]{3,2,1,0:T(8,128)(2,1)S(1)}, bf16[4,4,16,128]{3,2,1,0:T(8,128)(2,1)S(1)}, u32[]{:S(2)}, u32[]{:S(2)}) collective-permute-start(bf16[4,4,16,128]{3,2,1,0:T(8,128)(2,1)S(1)} %bitcast.97), channel_id=1, source_target_pairs={{0,32},{32,0},{64,96},{96,64},{128,160},{160,128},{192,224},{224,1... | collective-permute-start | bytes 196616 | tf_op jit(solution)/shard_map/ppermute | solution.py:76
  18.9 5.3 %collective-permute-start.10 = (bf16[4,4,16,128]{3,2,1,0:T(8,128)(2,1)S(1)}, bf16[4,4,16,128]{3,2,1,0:T(8,128)(2,1)S(1)}, u32[]{:S(2)}, u32[]{:S(2)}) collective-permute-start(bf16[4,4,16,128]{3,2,1,0:T(8,128)(2,1)S(1)} %bitcast.99), channel_id=1, source_target_pairs={{0,4},{1,5},{2,6},{3,7},{4,0},{5,1},{6,2},{7,3},{8,12},{9,13},{10,... | collective-permute-start | bytes 196616 | tf_op jit(solution)/shard_map/ppermute | solution.py:76
  24.2 10.1 %collective-permute-start.11 = (bf16[8,4,16,128]{3,2,1,0:T(8,128)(2,1)S(1)}, bf16[8,4,16,128]{3,2,1,0:T(8,128)(2,1)S(1)}, u32[]{:S(2)}, u32[]{:S(2)}) collective-permute-start(bf16[8,4,16,128]{3,2,1,0:T(8,128)(2,1)S(1)} %bitcast.86), channel_id=1, source_target_pairs={{0,2},{1,3},{2,0},{3,1},{4,6},{5,7},{6,4},{7,5},{8,10},{9,11},{10,... | collective-permute-start | bytes 393224 | tf_op jit(solution)/shard_map/ppermute | solution.py:76
  33.0 12.4 %copy-start = (f32[128,16,128]{2,1,0:T(8,128)S(1)}, f32[128,16,128]{2,1,0:T(8,128)}, u32[]{:S(2)}) copy-start(f32[128,16,128]{2,1,0:T(8,128)} %shard_map.46) | copy-start | bytes 3145732
  34.2 11.3 %collective-permute-start.3 = (f32[16,4,16,128]{3,2,1,0:T(8,128)S(1)}, f32[16,4,16,128]{3,2,1,0:T(8,128)S(1)}, u32[]{:S(2)}, u32[]{:S(2)}) collective-permute-start(f32[16,4,16,128]{3,2,1,0:T(8,128)S(1)} %dynamic-slice_bitcast_fusion), channel_id=1, source_target_pairs={{0,1},{1,0},{2,3},{3,2},{4,5},{5,4},{6,7},{7,6},{8,9},{9,8},{10,11... | collective-permute-start | bytes 1572872 | tf_op jit(solution)/shard_map/ppermute | solution.py:92
  34.3 2.2 %collective-permute-start.12 = (bf16[16,4,16,128]{3,2,1,0:T(8,128)(2,1)S(1)}, bf16[16,4,16,128]{3,2,1,0:T(8,128)(2,1)S(1)}, u32[]{:S(2)}, u32[]{:S(2)}) collective-permute-start(bf16[16,4,16,128]{3,2,1,0:T(8,128)(2,1)S(1)} %bitcast.81), channel_id=1, source_target_pairs={{0,1},{1,0},{2,3},{3,2},{4,5},{5,4},{6,7},{7,6},{8,9},{9,8},{10,11... | collective-permute-start | bytes 786440 | tf_op jit(solution)/shard_map/ppermute | solution.py:76
  43.8 5.6 %collective-permute-start.13 = (f32[4,4,16,128]{3,2,1,0:T(8,128)S(1)}, f32[4,4,16,128]{3,2,1,0:T(8,128)S(1)}, u32[]{:S(2)}, u32[]{:S(2)}) collective-permute-start(f32[4,4,16,128]{3,2,1,0:T(8,128)S(1)} %dynamic-slice_bitcast_fusion.2), channel_id=1, source_target_pairs={{0,32},{32,0},{64,96},{96,64},{128,160},{160,128},{192,224},{224,1... | collective-permute-start | bytes 393224 | tf_op jit(solution)/shard_map/ppermute | solution.py:92
  45.5 8.2 %collective-permute-start.4 = (f32[8,4,16,128]{3,2,1,0:T(8,128)S(1)}, f32[8,4,16,128]{3,2,1,0:T(8,128)S(1)}, u32[]{:S(2)}, u32[]{:S(2)}) collective-permute-start(f32[8,4,16,128]{3,2,1,0:T(8,128)S(1)} %dynamic-slice_bitcast_fusion.1), channel_id=1, source_target_pairs={{0,2},{1,3},{2,0},{3,1},{4,6},{5,7},{6,4},{7,5},{8,10},{9,11},{10,... | collective-permute-start | bytes 786440 | tf_op jit(solution)/shard_map/ppermute | solution.py:92
  50.4 6.7 %collective-permute-start.14 = (f32[2,4,16,128]{3,2,1,0:T(8,128)S(1)}, f32[2,4,16,128]{3,2,1,0:T(8,128)S(1)}, u32[]{:S(2)}, u32[]{:S(2)}) collective-permute-start(f32[2,4,16,128]{3,2,1,0:T(8,128)S(1)} %dynamic-slice_bitcast_fusion.4), channel_id=1, source_target_pairs={{0,64},{32,96},{64,0},{96,32},{128,192},{160,224},{192,128},{224,1... | collective-permute-start | bytes 196616 | tf_op jit(solution)/shard_map/ppermute | solution.py:92
  53.8 8.7 %collective-permute-start.5 = (f32[4,4,16,128]{3,2,1,0:T(8,128)S(1)}, f32[4,4,16,128]{3,2,1,0:T(8,128)S(1)}, u32[]{:S(2)}, u32[]{:S(2)}) collective-permute-start(f32[4,4,16,128]{3,2,1,0:T(8,128)S(1)} %dynamic-slice_bitcast_fusion.3), channel_id=1, source_target_pairs={{0,4},{1,5},{2,6},{3,7},{4,0},{5,1},{6,2},{7,3},{8,12},{9,13},{10,... | collective-permute-start | bytes 393224 | tf_op jit(solution)/shard_map/ppermute | solution.py:92
  62.5 8.3 %collective-permute-start.6 = (f32[2,4,16,128]{3,2,1,0:T(8,128)S(1)}, f32[2,4,16,128]{3,2,1,0:T(8,128)S(1)}, u32[]{:S(2)}, u32[]{:S(2)}) collective-permute-start(f32[2,4,16,128]{3,2,1,0:T(8,128)S(1)} %dynamic-slice_bitcast_fusion.5), channel_id=1, source_target_pairs={{0,8},{1,9},{2,10},{3,11},{4,12},{5,13},{6,14},{7,15},{8,0},{9,1},... | collective-permute-start | bytes 196616 | tf_op jit(solution)/shard_map/ppermute | solution.py:92
  68.4 5.4 %collective-permute-start.15 = (f32[1,4,16,128]{3,2,1,0:T(8,128)S(1)}, f32[1,4,16,128]{3,2,1,0:T(8,128)S(1)}, u32[]{:S(2)}, u32[]{:S(2)}) collective-permute-start(f32[1,4,16,128]{3,2,1,0:T(8,128)S(1)} %constant_dynamic-slice_fusion.1), channel_id=1, source_target_pairs={{0,128},{32,160},{64,192},{96,224},{128,0},{160,32},{192,64},{224,... | collective-permute-start | bytes 98312 | tf_op jit(solution)/shard_map/ppermute | solution.py:92
  70.8 5.5 %collective-permute-start.7 = (f32[1,4,16,128]{3,2,1,0:T(8,128)S(1)}, f32[1,4,16,128]{3,2,1,0:T(8,128)S(1)}, u32[]{:S(2)}, u32[]{:S(2)}) collective-permute-start(f32[1,4,16,128]{3,2,1,0:T(8,128)S(1)} %constant_dynamic-slice_fusion), channel_id=1, source_target_pairs={{0,16},{1,17},{2,18},{3,19},{4,20},{5,21},{6,22},{7,23},{8,24},{9,... | collective-permute-start | bytes 98312 | tf_op jit(solution)/shard_map/ppermute | solution.py:92

commit v5 on v4

--- a/solution.py
+++ b/solution.py
@@ -93,6 +93,18 @@
     return buf.reshape(seg_blocks, *x.shape[1:])
 
 
+def scatter_a2a(x, axis, seg_blocks):
+    n = lax.axis_size(axis)
+    y = lax.all_to_all(x, axis, 0, 0, tiled=True)
+    return y.reshape(n, seg_blocks, *x.shape[1:]).sum(0)
+
+
+def gather_a2a(own, axis):
+    n = lax.axis_size(axis)
+    y = jnp.broadcast_to(own[None], (n,) + own.shape).reshape(n * own.shape[0], *own.shape[1:])
+    return lax.all_to_all(y, axis, 0, 0, tiled=True)
+
+
 def body(vectors, blocks, row_ptr, col_idx):
     count_vectors = vectors.shape[0]
     segment = vectors.shape[1]
@@ -118,7 +130,7 @@
     forward_sum = tile_apply(slot_rows, columns, count, tile_blocks, col_side, tile_rows, True)
     forward_part = scatter_sum(forward_sum, "col", seg_blocks)
     backward_sum = tile_apply(slot_rows, columns, count, tile_blocks, row_side, tile_cols, False)
-    backward_part = scatter_sum(backward_sum, "row", seg_blocks)
+    backward_part = scatter_a2a(backward_sum, "row", seg_blocks)
     combined = forward_part + backward_part
     return combined.transpose(1, 0, 2).reshape(count_vectors, segment)
 

time: 77.1 us -> 75.3 us (0.977)
  starting transfers between devices: 34.8 us -> 33.4 us
  local copies, waits for them, and re-layouts: 4.49 us -> 3.41 us
    ppermute x8 -> x5, waiting for transfers between devices: 16.3 us -> 5.2 us  [scatter_sum(): buf = keep + lax.ppermute(send, axis, [(i, i ^ 1 << b) for i in range(n)])]
    ppermute x8, waiting for transfers between devices: 5.13 us -> 13.8 us  [gather_blocks(): recv = lax.ppermute(buf, axis, [(i, i ^ 1 << b) for i in range(n)])]
    ppermute x8 -> x5, starting transfers between devices: 15.1 us -> 7.55 us  [scatter_sum(): buf = keep + lax.ppermute(send, axis, [(i, i ^ 1 << b) for i in range(n)])]
    all_to_all x0 -> x1, starting transfers between devices: none -> 4.75 us  [scatter_a2a(): y = lax.all_to_all(x, axis, 0, 0, tiled=True)]
    all_to_all x0 -> x1, waiting for transfers between devices: none -> 2.36 us  [scatter_a2a(): y = lax.all_to_all(x, axis, 0, 0, tiled=True)]
    ppermute x8, starting transfers between devices: 19.7 us -> 21.1 us  [gather_blocks(): recv = lax.ppermute(buf, axis, [(i, i ^ 1 << b) for i in range(n)])]
    squeeze x8 -> x5, local copies, waits for them, and re-layouts: 2.17 us -> 1.15 us  [scatter_sum(): send = lax.dynamic_index_in_dim(buf, 1 - bit, 1, keepdims=False)]
  transfers between devices with their start and end apart: 16 -> 14, of which waited for: 11 -> 8; matrix products, arithmetic and copies ran while one was open for 8% -> 5% of each run, Pallas kernels for 16% -> 7%
where the time goes in v5:
time: 75.3 us; the launch traced here: 74.6 us
  starting transfers between devices  33.4 us (44%)
  waiting for transfers between devices  21.4 us (28%)
  Pallas kernels  12.7 us (17%)
  other arithmetic  3.5 us (5%)
  local copies, waits for them, and re-layouts  3.41 us (5%)
    ppermute x8, starting transfers between devices, gather_blocks(): recv = lax.ppermute(buf, axis, [(i, i ^ 1 << b) for i in range(n)])  21.1 us
    ppermute x8, waiting for transfers between devices, gather_blocks(): recv = lax.ppermute(buf, axis, [(i, i ^ 1 << b) for i in range(n)])  13.8 us
    pallas_call x2, Pallas kernels, tile_apply(): pl.pallas_call(kernel, grid_spec=grid_spec, out_shape=jax.ShapeDtypeStruc...  12.7 us
    ppermute x5, starting transfers between devices, scatter_sum(): buf = keep + lax.ppermute(send, axis, [(i, i ^ 1 << b) for i in range(n)])  7.55 us
    ppermute x5, waiting for transfers between devices, scatter_sum(): buf = keep + lax.ppermute(send, axis, [(i, i ^ 1 << b) for i in range(n)])  5.2 us
    all_to_all x1, starting transfers between devices, scatter_a2a(): y = lax.all_to_all(x, axis, 0, 0, tiled=True)  4.75 us
    all_to_all x1, waiting for transfers between devices, scatter_a2a(): y = lax.all_to_all(x, axis, 0, 0, tiled=True)  2.36 us
    select_n x6, local copies, waits for them, and re-layouts, gather_blocks(): buf = jnp.where(low, jnp.stack([buf, recv], 1), jnp.stack([recv, buf], 1))  1.53 us
  transfers between devices with their start and end apart: 14, of which 8 were waited for; matrix products, arithmetic and copies ran while one was open for 5% of the time, Pallas kernels for 7%

profile of v5, /device:TPU:8, one launch (start us, length us, event | category | flops | bytes accessed | tf_op | source)
XLA Modules:
  0.0 74.6 jit_solution(13357193223610201579)
XLA Ops:
  0.0 0.7 reshape.292
  0.7 2.3 %collective-permute-start = (bf16[1,4,16,128]{3,1,2,0:T(4,128)(2,1)S(1)}, bf16[1,4,16,128]{3,1,2,0:T(4,128)(2,1)S(1)}, u32[]{:S(2)}, u32[]{:S(2)}) collective-permute-start(bf16[1,4,16,128]{3,1,2,0:T(4,128)(2,1)S(1)} %bitcast.83), channel_id=1, source_target_pairs={{0,128},{32,160},{64,192},{96,224},{128,0},{160,32},{192,64},{224,... | collective-permute-start | bytes 49160 | tf_op jit(solution)/shard_map/ppermute | solution.py:76
  3.0 3.0 %collective-permute-start.8 = (bf16[1,4,16,128]{3,1,2,0:T(4,128)(2,1)S(1)}, bf16[1,4,16,128]{3,1,2,0:T(4,128)(2,1)S(1)}, u32[]{:S(2)}, u32[]{:S(2)}) collective-permute-start(bf16[1,4,16,128]{3,1,2,0:T(4,128)(2,1)S(1)} %bitcast.84), channel_id=1, source_target_pairs={{0,16},{1,17},{2,18},{3,19},{4,20},{5,21},{6,22},{7,23},{8,24},{9,... | collective-permute-start | bytes 49160 | tf_op jit(solution)/shard_map/ppermute | solution.py:76
  6.0 0.8 %convert_reduce_fusion = s32[192]{0:T(256)S(1)} fusion(s32[129]{0:T(256)} %bitcast.101), kind=kLoop, calls=%fused_computation.6 | loop fusion | flops 74112 | bytes 1284 | tf_op jit(solution)/shard_map/reduce_sum | solution.py:121
  6.9 1.4 %collective-permute-done.8 = bf16[1,4,16,128]{3,1,2,0:T(4,128)(2,1)S(1)} collective-permute-done((bf16[1,4,16,128]{3,1,2,0:T(4,128)(2,1)S(1)}, bf16[1,4,16,128]{3,1,2,0:T(4,128)(2,1)S(1)}, u32[]{:S(2)}, u32[]{:S(2)}) %collective-permute-start.8) | collective-permute-done | bytes 16416 | tf_op jit(solution)/shard_map/ppermute | solution.py:76
  8.3 1.4 %collective-permute-start.1 = (bf16[2,4,16,128]{3,1,2,0:T(4,128)(2,1)S(1)}, bf16[2,4,16,128]{3,1,2,0:T(4,128)(2,1)S(1)}, u32[]{:S(2)}, u32[]{:S(2)}) collective-permute-start(bf16[2,4,16,128]{3,1,2,0:T(4,128)(2,1)S(1)} %get-tuple-element.7), channel_id=1, source_target_pairs={{0,64},{32,96},{64,0},{96,32},{128,192},{160,224},{192,128},{224,1... | collective-permute-start | bytes 98312 | tf_op jit(solution)/shard_map/ppermute | solution.py:76
  9.8 2.5 %collective-permute-done.1 = bf16[2,4,16,128]{3,1,2,0:T(4,128)(2,1)S(1)} collective-permute-done((bf16[2,4,16,128]{3,1,2,0:T(4,128)(2,1)S(1)}, bf16[2,4,16,128]{3,1,2,0:T(4,128)(2,1)S(1)}, u32[]{:S(2)}, u32[]{:S(2)}) %collective-permute-start.1) | collective-permute-done | bytes 32800 | tf_op jit(solution)/shard_map/ppermute | solution.py:76
  12.4 1.6 %collective-permute-start.2 = (bf16[4,4,16,128]{3,2,1,0:T(8,128)(2,1)S(1)}, bf16[4,4,16,128]{3,2,1,0:T(8,128)(2,1)S(1)}, u32[]{:S(2)}, u32[]{:S(2)}) collective-permute-start(bf16[4,4,16,128]{3,2,1,0:T(8,128)(2,1)S(1)} %bitcast.88), channel_id=1, source_target_pairs={{0,32},{32,0},{64,96},{96,64},{128,160},{160,128},{192,224},{224,1... | collective-permute-start | bytes 196616 | tf_op jit(solution)/shard_map/ppermute | solution.py:76
  14.0 0.6 add_minimum_fusion.rows_ref
  14.5 2.2 %collective-permute-done.2 = bf16[4,4,16,128]{3,2,1,0:T(8,128)(2,1)S(1)} collective-permute-done((bf16[4,4,16,128]{3,2,1,0:T(8,128)(2,1)S(1)}, bf16[4,4,16,128]{3,2,1,0:T(8,128)(2,1)S(1)}, u32[]{:S(2)}, u32[]{:S(2)}) %collective-permute-start.2) | collective-permute-done | bytes 65568 | tf_op jit(solution)/shard_map/ppermute | solution.py:76
  16.8 0.6 copy.38
  17.4 7.3 %shard_map.46 = f32[128,16,128]{2,1,0:T(8,128)} custom-call(s32[192]{0:T(256)} %add_minimum_fusion.rows_ref, s32[192]{0:T(256)} %bitcast.104, s32[129]{0:T(256)} %bitcast.102, bf16[192,128,128]{2,1,0:T(8,128)(2,1)} %bitcast.66, bf16[32,16,128]{2,1,0:T(8,128)(2,1)} %bitcast.78), custom_call_target="tpu_custom_call" | custom-call | flops 100663296 | bytes 7340032 | tf_op jit(solution)/shard_map/pallas_call | solution.py:52
  24.7 1.1 %dynamic-slice_bitcast_fusion = f32[16,4,16,128]{3,2,1,0:T(8,128)S(1)} fusion(f32[16,2,4,16,128]{4,3,2,1,0:T(8,128)} %bitcast.68, s32[]{:T(128)S(6)} %select_n.197), kind=kLoop, calls=%fused_computation.2 | loop fusion | bytes 1048580 | tf_op jit(solution)/shard_map/jit(dynamic_index_in_dim)/squeeze | solution.py:91
  25.8 0.1 collective-permute-start.3
  25.9 7.3 %collective-permute-start.9 = (bf16[2,4,16,128]{3,1,2,0:T(4,128)(2,1)S(1)}, bf16[2,4,16,128]{3,1,2,0:T(4,128)(2,1)S(1)}, u32[]{:S(2)}, u32[]{:S(2)}) collective-permute-start(bf16[2,4,16,128]{3,1,2,0:T(4,128)(2,1)S(1)} %get-tuple-element.8), channel_id=1, source_target_pairs={{0,8},{1,9},{2,10},{3,11},{4,12},{5,13},{6,14},{7,15},{8,0},{9,1},... | collective-permute-start | bytes 98312 | tf_op jit(solution)/shard_map/ppermute | solution.py:76
  33.2 1.1 %bitcast_add_fusion = f32[16,4,16,128]{3,2,1,0:T(8,128)S(1)} fusion(f32[16,4,16,128]{3,2,1,0:T(8,128)S(1)} %collective-permute-done.3, f32[16,2,4,16,128]{4,3,2,1,0:T(8,128)} %bitcast.69, s32[]{:T(128)S(6)} %select_n.196), kind=kLoop, calls=%fused_computation.1 | loop fusion | flops 131072 | bytes 1572868 | tf_op jit(solution)/shard_map/add | solution.py:92
  34.3 1.1 %collective-permute-start.4 = (f32[8,4,16,128]{3,2,1,0:T(8,128)S(1)}, f32[8,4,16,128]{3,2,1,0:T(8,128)S(1)}, u32[]{:S(2)}, u32[]{:S(2)}) collective-permute-start(f32[8,4,16,128]{3,2,1,0:T(8,128)S(1)} %dynamic-slice_bitcast_fusion.1), channel_id=1, source_target_pairs={{0,2},{1,3},{2,0},{3,1},{4,6},{5,7},{6,4},{7,5},{8,10},{9,11},{10,... | collective-permute-start | bytes 786440 | tf_op jit(solution)/shard_map/ppermute | solution.py:92
  35.5 2.4 %collective-permute-start.10 = (bf16[4,4,16,128]{3,2,1,0:T(8,128)(2,1)S(1)}, bf16[4,4,16,128]{3,2,1,0:T(8,128)(2,1)S(1)}, u32[]{:S(2)}, u32[]{:S(2)}) collective-permute-start(bf16[4,4,16,128]{3,2,1,0:T(8,128)(2,1)S(1)} %bitcast.90), channel_id=1, source_target_pairs={{0,4},{1,5},{2,6},{3,7},{4,0},{5,1},{6,2},{7,3},{8,12},{9,13},{10,... | collective-permute-start | bytes 196616 | tf_op jit(solution)/shard_map/ppermute | solution.py:76
  37.9 4.8 %collective-permute-done.10 = bf16[4,4,16,128]{3,2,1,0:T(8,128)(2,1)S(1)} collective-permute-done((bf16[4,4,16,128]{3,2,1,0:T(8,128)(2,1)S(1)}, bf16[4,4,16,128]{3,2,1,0:T(8,128)(2,1)S(1)}, u32[]{:S(2)}, u32[]{:S(2)}) %collective-permute-start.10) | collective-permute-done | bytes 65568 | tf_op jit(solution)/shard_map/ppermute | solution.py:76
  42.7 3.0 %collective-permute-start.11 = (bf16[8,4,16,128]{3,2,1,0:T(8,128)(2,1)S(1)}, bf16[8,4,16,128]{3,2,1,0:T(8,128)(2,1)S(1)}, u32[]{:S(2)}, u32[]{:S(2)}) collective-permute-start(bf16[8,4,16,128]{3,2,1,0:T(8,128)(2,1)S(1)} %bitcast.79), channel_id=1, source_target_pairs={{0,2},{1,3},{2,0},{3,1},{4,6},{5,7},{6,4},{7,5},{8,10},{9,11},{10,... | collective-permute-start | bytes 393224 | tf_op jit(solution)/shard_map/ppermute | solution.py:76
  45.8 0.6 collective-permute-start.5
  46.4 2.9 %collective-permute-done.11 = bf16[8,4,16,128]{3,2,1,0:T(8,128)(2,1)S(1)} collective-permute-done((bf16[8,4,16,128]{3,2,1,0:T(8,128)(2,1)S(1)}, bf16[8,4,16,128]{3,2,1,0:T(8,128)(2,1)S(1)}, u32[]{:S(2)}, u32[]{:S(2)}) %collective-permute-start.11) | collective-permute-done | bytes 131104 | tf_op jit(solution)/shard_map/ppermute | solution.py:76
  49.3 0.1 collective-permute-start.12
  49.4 4.2 %collective-permute-done.5 = f32[4,4,16,128]{3,2,1,0:T(8,128)S(1)} collective-permute-done((f32[4,4,16,128]{3,2,1,0:T(8,128)S(1)}, f32[4,4,16,128]{3,2,1,0:T(8,128)S(1)}, u32[]{:S(2)}, u32[]{:S(2)}) %collective-permute-start.5) | collective-permute-done | bytes 131104 | tf_op jit(solution)/shard_map/ppermute | solution.py:92
  53.7 2.6 %collective-permute-start.6 = (f32[2,4,16,128]{3,2,1,0:T(8,128)S(1)}, f32[2,4,16,128]{3,2,1,0:T(8,128)S(1)}, u32[]{:S(2)}, u32[]{:S(2)}) collective-permute-start(f32[2,4,16,128]{3,2,1,0:T(8,128)S(1)} %dynamic-slice_bitcast_fusion.3), channel_id=1, source_target_pairs={{0,8},{1,9},{2,10},{3,11},{4,12},{5,13},{6,14},{7,15},{8,0},{9,1},... | collective-permute-start | bytes 196616 | tf_op jit(solution)/shard_map/ppermute | solution.py:92
  56.4 0.8 %copy.45 = bf16[16,2,4,16,128]{4,3,2,1,0:T(8,128)(2,1)} copy(bf16[16,2,4,16,128]{4,3,2,0,1:T(8,128)(2,1)S(1)} %maximum_select_fusion) | data formatting | bytes 1048576 | tf_op jit(solution)/shard_map/jit(_where)/select_n | solution.py:78
  57.3 5.4 %shard_map.47 = f32[32,16,128]{2,1,0:T(8,128)} custom-call(s32[192]{0:T(256)} %add_minimum_fusion.rows_ref, s32[192]{0:T(256)} %bitcast.105, s32[129]{0:T(256)} %bitcast.103, bf16[192,128,128]{2,1,0:T(8,128)(2,1)} %bitcast.67, bf16[128,16,128]{2,1,0:T(8,128)(2,1)} %bitcast.72), custom_call_target="tpu_custom_call" | custom-call | flops 100663296 | bytes 6553600 | tf_op jit(solution)/shard_map/pallas_call | solution.py:52
  62.6 4.7 %all-to-all-start = ((f32[32,16,128]{2,1,0:T(8,128)}), f32[32,16,128]{2,1,0:T(8,128)S(1)}, u32[]{:S(2)}, u32[]{:S(2)}) async-start(f32[32,16,128]{2,1,0:T(8,128)} %shard_map.47), calls=%async_computation | async-start | bytes 524288 | tf_op jit(solution)/shard_map/all_to_all | solution.py:98
  67.4 3.1 %collective-permute-start.7 = (f32[1,4,16,128]{3,2,1,0:T(8,128)S(1)}, f32[1,4,16,128]{3,2,1,0:T(8,128)S(1)}, u32[]{:S(2)}, u32[]{:S(2)}) collective-permute-start(f32[1,4,16,128]{3,2,1,0:T(8,128)S(1)} %constant_dynamic-slice_fusion), channel_id=1, source_target_pairs={{0,16},{1,17},{2,18},{3,19},{4,20},{5,21},{6,22},{7,23},{8,24},{9,... | collective-permute-start | bytes 98312 | tf_op jit(solution)/shard_map/ppermute | solution.py:92
  70.6 2.4 %all-to-all-done = f32[32,16,128]{2,1,0:T(8,128)S(1)} async-done(((f32[32,16,128]{2,1,0:T(8,128)}), f32[32,16,128]{2,1,0:T(8,128)S(1)}, u32[]{:S(2)}, u32[]{:S(2)}) %all-to-all-start) | async-done | bytes 262176 | tf_op jit(solution)/shard_map/all_to_all | solution.py:98
  72.9 1.0 %collective-permute-done.7 = f32[1,4,16,128]{3,2,1,0:T(8,128)S(1)} collective-permute-done((f32[1,4,16,128]{3,2,1,0:T(8,128)S(1)}, f32[1,4,16,128]{3,2,1,0:T(8,128)S(1)}, u32[]{:S(2)}, u32[]{:S(2)}) %collective-permute-start.7) | collective-permute-done | bytes 32800 | tf_op jit(solution)/shard_map/ppermute | solution.py:92
  73.9 0.6 copy_bitcast_fusion
  (26 shorter events, 0.6 us)
Async XLA Ops:
  0.7 6.1 %collective-permute-start = (bf16[1,4,16,128]{3,1,2,0:T(4,128)(2,1)S(1)}, bf16[1,4,16,128]{3,1,2,0:T(4,128)(2,1)S(1)}, u32[]{:S(2)}, u32[]{:S(2)}) collective-permute-start(bf16[1,4,16,128]{3,1,2,0:T(4,128)(2,1)S(1)} %bitcast.83), channel_id=1, source_target_pairs={{0,128},{32,160},{64,192},{96,224},{128,0},{160,32},{192,64},{224,... | collective-permute-start | bytes 49160 | tf_op jit(solution)/shard_map/ppermute | solution.py:76
  3.0 5.2 %collective-permute-start.8 = (bf16[1,4,16,128]{3,1,2,0:T(4,128)(2,1)S(1)}, bf16[1,4,16,128]{3,1,2,0:T(4,128)(2,1)S(1)}, u32[]{:S(2)}, u32[]{:S(2)}) collective-permute-start(bf16[1,4,16,128]{3,1,2,0:T(4,128)(2,1)S(1)} %bitcast.84), channel_id=1, source_target_pairs={{0,16},{1,17},{2,18},{3,19},{4,20},{5,21},{6,22},{7,23},{8,24},{9,... | collective-permute-start | bytes 49160 | tf_op jit(solution)/shard_map/ppermute | solution.py:76
  8.3 4.0 %collective-permute-start.1 = (bf16[2,4,16,128]{3,1,2,0:T(4,128)(2,1)S(1)}, bf16[2,4,16,128]{3,1,2,0:T(4,128)(2,1)S(1)}, u32[]{:S(2)}, u32[]{:S(2)}) collective-permute-start(bf16[2,4,16,128]{3,1,2,0:T(4,128)(2,1)S(1)} %get-tuple-element.7), channel_id=1, source_target_pairs={{0,64},{32,96},{64,0},{96,32},{128,192},{160,224},{192,128},{224,1... | collective-permute-start | bytes 98312 | tf_op jit(solution)/shard_map/ppermute | solution.py:76
  12.4 4.4 %collective-permute-start.2 = (bf16[4,4,16,128]{3,2,1,0:T(8,128)(2,1)S(1)}, bf16[4,4,16,128]{3,2,1,0:T(8,128)(2,1)S(1)}, u32[]{:S(2)}, u32[]{:S(2)}) collective-permute-start(bf16[4,4,16,128]{3,2,1,0:T(8,128)(2,1)S(1)} %bitcast.88), channel_id=1, source_target_pairs={{0,32},{32,0},{64,96},{96,64},{128,160},{160,128},{192,224},{224,1... | collective-permute-start | bytes 196616 | tf_op jit(solution)/shard_map/ppermute | solution.py:76
  25.8 7.4 %collective-permute-start.3 = (f32[16,4,16,128]{3,2,1,0:T(8,128)S(1)}, f32[16,4,16,128]{3,2,1,0:T(8,128)S(1)}, u32[]{:S(2)}, u32[]{:S(2)}) collective-permute-start(f32[16,4,16,128]{3,2,1,0:T(8,128)S(1)} %dynamic-slice_bitcast_fusion), channel_id=1, source_target_pairs={{0,1},{1,0},{2,3},{3,2},{4,5},{5,4},{6,7},{7,6},{8,9},{9,8},{10,11... | collective-permute-start | bytes 1572872 | tf_op jit(solution)/shard_map/ppermute | solution.py:92
  25.9 9.5 %collective-permute-start.9 = (bf16[2,4,16,128]{3,1,2,0:T(4,128)(2,1)S(1)}, bf16[2,4,16,128]{3,1,2,0:T(4,128)(2,1)S(1)}, u32[]{:S(2)}, u32[]{:S(2)}) collective-permute-start(bf16[2,4,16,128]{3,1,2,0:T(4,128)(2,1)S(1)} %get-tuple-element.8), channel_id=1, source_target_pairs={{0,8},{1,9},{2,10},{3,11},{4,12},{5,13},{6,14},{7,15},{8,0},{9,1},... | collective-permute-start | bytes 98312 | tf_op jit(solution)/shard_map/ppermute | solution.py:76
  34.3 11.4 %collective-permute-start.4 = (f32[8,4,16,128]{3,2,1,0:T(8,128)S(1)}, f32[8,4,16,128]{3,2,1,0:T(8,128)S(1)}, u32[]{:S(2)}, u32[]{:S(2)}) collective-permute-start(f32[8,4,16,128]{3,2,1,0:T(8,128)S(1)} %dynamic-slice_bitcast_fusion.1), channel_id=1, source_target_pairs={{0,2},{1,3},{2,0},{3,1},{4,6},{5,7},{6,4},{7,5},{8,10},{9,11},{10,... | collective-permute-start | bytes 786440 | tf_op jit(solution)/shard_map/ppermute | solution.py:92
  35.5 7.2 %collective-permute-start.10 = (bf16[4,4,16,128]{3,2,1,0:T(8,128)(2,1)S(1)}, bf16[4,4,16,128]{3,2,1,0:T(8,128)(2,1)S(1)}, u32[]{:S(2)}, u32[]{:S(2)}) collective-permute-start(bf16[4,4,16,128]{3,2,1,0:T(8,128)(2,1)S(1)} %bitcast.90), channel_id=1, source_target_pairs={{0,4},{1,5},{2,6},{3,7},{4,0},{5,1},{6,2},{7,3},{8,12},{9,13},{10,... | collective-permute-start | bytes 196616 | tf_op jit(solution)/shard_map/ppermute | solution.py:76
  42.7 6.6 %collective-permute-start.11 = (bf16[8,4,16,128]{3,2,1,0:T(8,128)(2,1)S(1)}, bf16[8,4,16,128]{3,2,1,0:T(8,128)(2,1)S(1)}, u32[]{:S(2)}, u32[]{:S(2)}) collective-permute-start(bf16[8,4,16,128]{3,2,1,0:T(8,128)(2,1)S(1)} %bitcast.79), channel_id=1, source_target_pairs={{0,2},{1,3},{2,0},{3,1},{4,6},{5,7},{6,4},{7,5},{8,10},{9,11},{10,... | collective-permute-start | bytes 393224 | tf_op jit(solution)/shard_map/ppermute | solution.py:76
  45.8 7.9 %collective-permute-start.5 = (f32[4,4,16,128]{3,2,1,0:T(8,128)S(1)}, f32[4,4,16,128]{3,2,1,0:T(8,128)S(1)}, u32[]{:S(2)}, u32[]{:S(2)}) collective-permute-start(f32[4,4,16,128]{3,2,1,0:T(8,128)S(1)} %dynamic-slice_bitcast_fusion.2), channel_id=1, source_target_pairs={{0,4},{1,5},{2,6},{3,7},{4,0},{5,1},{6,2},{7,3},{8,12},{9,13},{10,... | collective-permute-start | bytes 393224 | tf_op jit(solution)/shard_map/ppermute | solution.py:92
  49.3 7.0 %collective-permute-start.12 = (bf16[16,4,16,128]{3,2,1,0:T(8,128)(2,1)S(1)}, bf16[16,4,16,128]{3,2,1,0:T(8,128)(2,1)S(1)}, u32[]{:S(2)}, u32[]{:S(2)}) collective-permute-start(bf16[16,4,16,128]{3,2,1,0:T(8,128)(2,1)S(1)} %bitcast.76), channel_id=1, source_target_pairs={{0,1},{1,0},{2,3},{3,2},{4,5},{5,4},{6,7},{7,6},{8,9},{9,8},{10,11... | collective-permute-start | bytes 786440 | tf_op jit(solution)/shard_map/ppermute | solution.py:76
  53.7 13.7 %collective-permute-start.6 = (f32[2,4,16,128]{3,2,1,0:T(8,128)S(1)}, f32[2,4,16,128]{3,2,1,0:T(8,128)S(1)}, u32[]{:S(2)}, u32[]{:S(2)}) collective-permute-start(f32[2,4,16,128]{3,2,1,0:T(8,128)S(1)} %dynamic-slice_bitcast_fusion.3), channel_id=1, source_target_pairs={{0,8},{1,9},{2,10},{3,11},{4,12},{5,13},{6,14},{7,15},{8,0},{9,1},... | collective-permute-start | bytes 196616 | tf_op jit(solution)/shard_map/ppermute | solution.py:92
  62.6 10.3 %all-to-all-start = ((f32[32,16,128]{2,1,0:T(8,128)}), f32[32,16,128]{2,1,0:T(8,128)S(1)}, u32[]{:S(2)}, u32[]{:S(2)}) async-start(f32[32,16,128]{2,1,0:T(8,128)} %shard_map.47), calls=%async_computation | async-start | bytes 524288 | tf_op jit(solution)/shard_map/all_to_all | solution.py:98
  67.4 6.5 %collective-permute-start.7 = (f32[1,4,16,128]{3,2,1,0:T(8,128)S(1)}, f32[1,4,16,128]{3,2,1,0:T(8,128)S(1)}, u32[]{:S(2)}, u32[]{:S(2)}) collective-permute-start(f32[1,4,16,128]{3,2,1,0:T(8,128)S(1)} %constant_dynamic-slice_fusion), channel_id=1, source_target_pairs={{0,16},{1,17},{2,18},{3,19},{4,20},{5,21},{6,22},{7,23},{8,24},{9,... | collective-permute-start | bytes 98312 | tf_op jit(solution)/shard_map/ppermute | solution.py:92

commit v6 on v5

--- a/solution.py
+++ b/solution.py
@@ -6,6 +6,7 @@
 from jax.experimental import pallas as pl
 from jax.experimental.pallas import tpu as pltpu
 from jax.sharding import PartitionSpec as P
+
 
 GROUP = 96
 
@@ -68,41 +69,46 @@
     return bits
 
 
-def gather_blocks(own, axis):
+def gather_blocks(own, axis, labels):
     n = lax.axis_size(axis)
-    me = lax.axis_index(axis)
+    back = {lab: i for i, lab in enumerate(labels)}
+    label = jnp.asarray(labels, jnp.int32)[lax.axis_index(axis)]
     buf = own[None]
     for b in reversed(range(_bits(n))):
-        recv = lax.ppermute(buf, axis, [(i, i ^ (1 << b)) for i in range(n)])
-        low = ((me >> b) & 1) == 0
+        pairs = [(i, back[labels[i] ^ (1 << b)]) for i in range(n)]
+        recv = lax.ppermute(buf, axis, pairs)
+        low = ((label >> b) & 1) == 0
         buf = jnp.where(low, jnp.stack([buf, recv], 1), jnp.stack([recv, buf], 1))
         buf = buf.reshape(-1, *own.shape)
     return buf.reshape(n * own.shape[0], *own.shape[1:])
 
 
-def scatter_sum(x, axis, seg_blocks):
+def scatter_sum(x, axis, seg_blocks, labels):
     n = lax.axis_size(axis)
-    me = lax.axis_index(axis)
+    back = {lab: i for i, lab in enumerate(labels)}
+    label = jnp.asarray(labels, jnp.int32)[lax.axis_index(axis)]
     buf = x.reshape(n, seg_blocks, *x.shape[1:])
     for b in range(_bits(n)):
         buf = buf.reshape(-1, 2, *buf.shape[1:])
-        bit = (me >> b) & 1
+        bit = (label >> b) & 1
         keep = lax.dynamic_index_in_dim(buf, bit, 1, keepdims=False)
         send = lax.dynamic_index_in_dim(buf, 1 - bit, 1, keepdims=False)
-        buf = keep + lax.ppermute(send, axis, [(i, i ^ (1 << b)) for i in range(n)])
+        pairs = [(i, back[labels[i] ^ (1 << b)]) for i in range(n)]
+        buf = keep + lax.ppermute(send, axis, pairs)
     return buf.reshape(seg_blocks, *x.shape[1:])
+
+
+def col_labels(n):
+    ring = (0, 1, 2, 3, 6, 7, 4, 5)
+    if n != 32:
+        return list(range(n))
+    return [(c // 16) * 16 + ring[(c // 2) % 8] * 2 + c % 2 for c in range(n)]
 
 
 def scatter_a2a(x, axis, seg_blocks):
     n = lax.axis_size(axis)
     y = lax.all_to_all(x, axis, 0, 0, tiled=True)
     return y.reshape(n, seg_blocks, *x.shape[1:]).sum(0)
-
-
-def gather_a2a(own, axis):
-    n = lax.axis_size(axis)
-    y = jnp.broadcast_to(own[None], (n,) + own.shape).reshape(n * own.shape[0], *own.shape[1:])
-    return lax.all_to_all(y, axis, 0, 0, tiled=True)
 
 
 def body(vectors, blocks, row_ptr, col_idx):
@@ -124,11 +130,16 @@
     count = pointers.astype(jnp.int32)
 
     own = vectors.reshape(count_vectors, seg_blocks, edge).transpose(1, 0, 2)
-    col_side = gather_blocks(own, "row")
-    row_side = gather_blocks(own, "col")
+    labels = col_labels(lax.axis_size("col"))
+    placed = jnp.asarray(
+        [labels[i // seg_blocks] * seg_blocks + i % seg_blocks for i in range(tile_rows)], jnp.int32
+    )
+    slot_rows = placed[slot_rows]
+    col_side = gather_blocks(own, "row", list(range(grid_rows)))
+    row_side = gather_blocks(own, "col", labels)
 
     forward_sum = tile_apply(slot_rows, columns, count, tile_blocks, col_side, tile_rows, True)
-    forward_part = scatter_sum(forward_sum, "col", seg_blocks)
+    forward_part = scatter_sum(forward_sum, "col", seg_blocks, labels)
     backward_sum = tile_apply(slot_rows, columns, count, tile_blocks, row_side, tile_cols, False)
     backward_part = scatter_a2a(backward_sum, "row", seg_blocks)
     combined = forward_part + backward_part
@@ -143,4 +154,5 @@
         P("row", "col"),
     )
     out_specs = P(None, ("row", "col"))
+
     return jax.shard_map(body, mesh=mesh, in_specs=in_specs, out_specs=out_specs, check_vma=False)

time: 75.3 us -> 74.9 us (level)
  the two profiles are of different devices: /device:TPU:8 before, /device:TPU:32 now
where the time goes in v6:
time: 74.9 us; the launch traced here: 74.5 us
  starting transfers between devices  27 us (36%)
  waiting for transfers between devices  21.8 us (29%)
  Pallas kernels  12.6 us (17%)
  local copies, waits for them, and re-layouts  7.08 us (9%)
  between operations  3 us (4%)
  other arithmetic  2.96 us (4%)
    ppermute x8, waiting for transfers between devices, gather_blocks(): recv = lax.ppermute(buf, axis, pairs)  15 us
    ppermute x8, starting transfers between devices, gather_blocks(): recv = lax.ppermute(buf, axis, pairs)  14.5 us
    pallas_call x2, Pallas kernels, tile_apply(): pl.pallas_call(kernel, grid_spec=grid_spec, out_shape=jax.ShapeDtypeStruc...  12.6 us
    ppermute x5, starting transfers between devices, scatter_sum(): buf = keep + lax.ppermute(send, axis, pairs)  9.02 us
    all_to_all x1, waiting for transfers between devices, scatter_a2a(): y = lax.all_to_all(x, axis, 0, 0, tiled=True)  4.95 us
    all_to_all x1, starting transfers between devices, scatter_a2a(): y = lax.all_to_all(x, axis, 0, 0, tiled=True)  3.41 us
    gather x1, local copies, waits for them, and re-layouts, body(): slot_rows = placed[slot_rows]  2.46 us
    ppermute x5, waiting for transfers between devices, scatter_sum(): buf = keep + lax.ppermute(send, axis, pairs)  1.82 us
  transfers between devices with their start and end apart: 14, of which 7 were waited for; matrix products, arithmetic and copies ran while one was open for 9% of the time, Pallas kernels for 7%

profile of v6, /device:TPU:32, one launch (start us, length us, event | category | flops | bytes accessed | tf_op | source)
XLA Modules:
  0.0 74.5 jit_solution(14345782105297383079)
XLA Ops:
  0.0 0.7 reshape.383
  0.7 3.2 %collective-permute-start = (bf16[1,4,16,128]{3,1,2,0:T(4,128)(2,1)S(1)}, bf16[1,4,16,128]{3,1,2,0:T(4,128)(2,1)S(1)}, u32[]{:S(2)}, u32[]{:S(2)}) collective-permute-start(bf16[1,4,16,128]{3,1,2,0:T(4,128)(2,1)S(1)} %bitcast.95), channel_id=1, source_target_pairs={{0,128},{32,160},{64,192},{96,224},{128,0},{160,32},{192,64},{224,... | collective-permute-start | bytes 49160 | tf_op jit(solution)/shard_map/ppermute | solution.py:79
  3.9 3.0 %collective-permute-start.8 = (bf16[1,4,16,128]{3,1,2,0:T(4,128)(2,1)S(1)}, bf16[1,4,16,128]{3,1,2,0:T(4,128)(2,1)S(1)}, u32[]{:S(2)}, u32[]{:S(2)}) collective-permute-start(bf16[1,4,16,128]{3,1,2,0:T(4,128)(2,1)S(1)} %bitcast.96), channel_id=1, source_target_pairs={{0,16},{1,17},{2,18},{3,19},{4,20},{5,21},{6,22},{7,23},{8,24},{9,... | collective-permute-start | bytes 49160 | tf_op jit(solution)/shard_map/ppermute | solution.py:79
  6.9 0.8 %convert_reduce_fusion = s32[192]{0:T(256)S(1)} fusion(s32[129]{0:T(256)} %bitcast.113), kind=kLoop, calls=%fused_computation.7 | loop fusion | flops 74112 | bytes 1284 | tf_op jit(solution)/shard_map/reduce_sum | solution.py:127
  7.8 1.2 %dynamic_slice.41 = s32[1]{0:T(128)} dynamic-slice(s32[32]{0:T(128)} %constant.113.clone, s32[]{:T(128)S(6)} %select_n.215), dynamic_slice_sizes={1} | dynamic-slice | bytes 12 | tf_op jit(solution)/shard_map/dynamic_slice | solution.py:89
  10.2 0.8 %collective-permute-start.1 = (bf16[2,4,16,128]{3,1,2,0:T(4,128)(2,1)S(1)}, bf16[2,4,16,128]{3,1,2,0:T(4,128)(2,1)S(1)}, u32[]{:S(2)}, u32[]{:S(2)}) collective-permute-start(bf16[2,4,16,128]{3,1,2,0:T(4,128)(2,1)S(1)} %get-tuple-element.7), channel_id=1, source_target_pairs={{0,64},{32,96},{64,0},{96,32},{128,192},{160,224},{192,128},{224,1... | collective-permute-start | bytes 98312 | tf_op jit(solution)/shard_map/ppermute | solution.py:79
  11.0 3.2 %collective-permute-done.1 = bf16[2,4,16,128]{3,1,2,0:T(4,128)(2,1)S(1)} collective-permute-done((bf16[2,4,16,128]{3,1,2,0:T(4,128)(2,1)S(1)}, bf16[2,4,16,128]{3,1,2,0:T(4,128)(2,1)S(1)}, u32[]{:S(2)}, u32[]{:S(2)}) %collective-permute-start.1) | collective-permute-done | bytes 32800 | tf_op jit(solution)/shard_map/ppermute | solution.py:79
  14.2 0.7 collective-permute-start.2
  14.9 2.5 %gather_fusion = s32[192]{0:T(256)} fusion(s32[128]{0:T(128)} %constant.112.clone, s32[1024]{0:T(1024)S(1)} %pad_clamp_fusion), kind=kCustom, calls=%fused_computation | custom fusion | bytes 2304 | tf_op jit(solution)/shard_map/gather | solution.py:137
  17.4 1.2 %collective-permute-done.2 = bf16[4,4,16,128]{3,2,1,0:T(8,128)(2,1)S(1)} collective-permute-done((bf16[4,4,16,128]{3,2,1,0:T(8,128)(2,1)S(1)}, bf16[4,4,16,128]{3,2,1,0:T(8,128)(2,1)S(1)}, u32[]{:S(2)}, u32[]{:S(2)}) %collective-permute-start.2) | collective-permute-done | bytes 65568 | tf_op jit(solution)/shard_map/ppermute | solution.py:79
  18.6 0.6 copy.42
  19.3 7.3 %shard_map.82 = f32[128,16,128]{2,1,0:T(8,128)} custom-call(s32[192]{0:T(256)} %gather_fusion, s32[192]{0:T(256)} %bitcast.116, s32[129]{0:T(256)} %bitcast.114, bf16[192,128,128]{2,1,0:T(8,128)(2,1)} %bitcast.78, bf16[32,16,128]{2,1,0:T(8,128)(2,1)} %bitcast.90), custom_call_target="tpu_custom_call" | custom-call | flops 100663296 | bytes 7340032 | tf_op jit(solution)/shard_map/pallas_call | solution.py:53
  26.5 1.1 %dynamic-slice_bitcast_fusion = f32[16,4,16,128]{3,2,1,0:T(8,128)S(1)} fusion(f32[16,2,4,16,128]{4,3,2,1,0:T(8,128)} %bitcast.80, s32[]{:T(128)S(6)} %select_n.217), kind=kLoop, calls=%fused_computation.3 | loop fusion | bytes 1048580 | tf_op jit(solution)/shard_map/jit(dynamic_index_in_dim)/squeeze | solution.py:95
  27.6 0.1 collective-permute-start.3
  28.8 5.5 %collective-permute-start.9 = (bf16[2,4,16,128]{3,1,2,0:T(4,128)(2,1)S(1)}, bf16[2,4,16,128]{3,1,2,0:T(4,128)(2,1)S(1)}, u32[]{:S(2)}, u32[]{:S(2)}) collective-permute-start(bf16[2,4,16,128]{3,1,2,0:T(4,128)(2,1)S(1)} %get-tuple-element.8), channel_id=1, source_target_pairs={{0,12},{1,13},{2,14},{3,15},{4,8},{5,9},{6,10},{7,11},{8,4},{9,5},... | collective-permute-start | bytes 98312 | tf_op jit(solution)/shard_map/ppermute | solution.py:79
  34.3 1.1 %bitcast_add_fusion = f32[16,4,16,128]{3,2,1,0:T(8,128)S(1)} fusion(f32[16,4,16,128]{3,2,1,0:T(8,128)S(1)} %collective-permute-done.3, f32[16,2,4,16,128]{4,3,2,1,0:T(8,128)} %bitcast.81, s32[]{:T(128)S(6)} %select_n.216), kind=kLoop, calls=%fused_computation.2 | loop fusion | flops 131072 | bytes 1572868 | tf_op jit(solution)/shard_map/add | solution.py:97
  35.4 1.1 %collective-permute-start.4 = (f32[8,4,16,128]{3,2,1,0:T(8,128)S(1)}, f32[8,4,16,128]{3,2,1,0:T(8,128)S(1)}, u32[]{:S(2)}, u32[]{:S(2)}) collective-permute-start(f32[8,4,16,128]{3,2,1,0:T(8,128)S(1)} %dynamic-slice_bitcast_fusion.1), channel_id=1, source_target_pairs={{0,2},{1,3},{2,0},{3,1},{4,6},{5,7},{6,4},{7,5},{8,10},{9,11},{10,... | collective-permute-start | bytes 786440 | tf_op jit(solution)/shard_map/ppermute | solution.py:97
  36.5 0.5 collective-permute-done.9
  37.1 1.2 %collective-permute-start.10 = (bf16[4,4,16,128]{3,2,1,0:T(8,128)(2,1)S(1)}, bf16[4,4,16,128]{3,2,1,0:T(8,128)(2,1)S(1)}, u32[]{:S(2)}, u32[]{:S(2)}) collective-permute-start(bf16[4,4,16,128]{3,2,1,0:T(8,128)(2,1)S(1)} %bitcast.100), channel_id=1, source_target_pairs={{0,4},{1,5},{2,6},{3,7},{4,0},{5,1},{6,2},{7,3},{8,12},{9,13},{10,... | collective-permute-start | bytes 196616 | tf_op jit(solution)/shard_map/ppermute | solution.py:79
  38.9 6.9 %collective-permute-done.10 = bf16[4,4,16,128]{3,2,1,0:T(8,128)(2,1)S(1)} collective-permute-done((bf16[4,4,16,128]{3,2,1,0:T(8,128)(2,1)S(1)}, bf16[4,4,16,128]{3,2,1,0:T(8,128)(2,1)S(1)}, u32[]{:S(2)}, u32[]{:S(2)}) %collective-permute-start.10) | collective-permute-done | bytes 65568 | tf_op jit(solution)/shard_map/ppermute | solution.py:79
  45.8 0.1 collective-permute-start.11
  46.0 2.5 %collective-permute-start.5 = (f32[4,4,16,128]{3,2,1,0:T(8,128)S(1)}, f32[4,4,16,128]{3,2,1,0:T(8,128)S(1)}, u32[]{:S(2)}, u32[]{:S(2)}) collective-permute-start(f32[4,4,16,128]{3,2,1,0:T(8,128)S(1)} %dynamic-slice_bitcast_fusion.2), channel_id=1, source_target_pairs={{0,4},{1,5},{2,6},{3,7},{4,0},{5,1},{6,2},{7,3},{8,12},{9,13},{10,... | collective-permute-start | bytes 393224 | tf_op jit(solution)/shard_map/ppermute | solution.py:97
  48.5 3.2 %collective-permute-done.11 = bf16[8,4,16,128]{3,2,1,0:T(8,128)(2,1)S(1)} collective-permute-done((bf16[8,4,16,128]{3,2,1,0:T(8,128)(2,1)S(1)}, bf16[8,4,16,128]{3,2,1,0:T(8,128)(2,1)S(1)}, u32[]{:S(2)}, u32[]{:S(2)}) %collective-permute-start.11) | collective-permute-done | bytes 131104 | tf_op jit(solution)/shard_map/ppermute | solution.py:79
  51.8 0.1 collective-permute-start.12
  51.9 1.8 %collective-permute-done.5 = f32[4,4,16,128]{3,2,1,0:T(8,128)S(1)} collective-permute-done((f32[4,4,16,128]{3,2,1,0:T(8,128)S(1)}, f32[4,4,16,128]{3,2,1,0:T(8,128)S(1)}, u32[]{:S(2)}, u32[]{:S(2)}) %collective-permute-start.5) | collective-permute-done | bytes 131104 | tf_op jit(solution)/shard_map/ppermute | solution.py:97
  53.8 3.1 %collective-permute-start.6 = (f32[2,4,16,128]{3,2,1,0:T(8,128)S(1)}, f32[2,4,16,128]{3,2,1,0:T(8,128)S(1)}, u32[]{:S(2)}, u32[]{:S(2)}) collective-permute-start(f32[2,4,16,128]{3,2,1,0:T(8,128)S(1)} %dynamic-slice_bitcast_fusion.3), channel_id=1, source_target_pairs={{0,12},{1,13},{2,14},{3,15},{4,8},{5,9},{6,10},{7,11},{8,4},{9,5},... | collective-permute-start | bytes 196616 | tf_op jit(solution)/shard_map/ppermute | solution.py:97
  56.9 0.8 %copy.49 = bf16[16,2,4,16,128]{4,3,2,1,0:T(8,128)(2,1)} copy(bf16[16,2,4,16,128]{4,3,2,0,1:T(8,128)(2,1)S(1)} %maximum_select_fusion) | data formatting | bytes 1048576 | tf_op jit(solution)/shard_map/jit(_where)/select_n | solution.py:81
  57.8 5.4 %shard_map.83 = f32[32,16,128]{2,1,0:T(8,128)} custom-call(s32[192]{0:T(256)} %gather_fusion, s32[192]{0:T(256)} %bitcast.117, s32[129]{0:T(256)} %bitcast.115, bf16[192,128,128]{2,1,0:T(8,128)(2,1)} %bitcast.79, bf16[128,16,128]{2,1,0:T(8,128)(2,1)} %bitcast.84), custom_call_target="tpu_custom_call" | custom-call | flops 100663296 | bytes 6553600 | tf_op jit(solution)/shard_map/pallas_call | solution.py:53
  63.2 3.4 %all-to-all-start = ((f32[32,16,128]{2,1,0:T(8,128)}), f32[32,16,128]{2,1,0:T(8,128)S(1)}, u32[]{:S(2)}, u32[]{:S(2)}) async-start(f32[32,16,128]{2,1,0:T(8,128)} %shard_map.83), calls=%async_computation | async-start | bytes 524288 | tf_op jit(solution)/shard_map/all_to_all | solution.py:110
  66.6 2.2 %collective-permute-start.7 = (f32[1,4,16,128]{3,2,1,0:T(8,128)S(1)}, f32[1,4,16,128]{3,2,1,0:T(8,128)S(1)}, u32[]{:S(2)}, u32[]{:S(2)}) collective-permute-start(f32[1,4,16,128]{3,2,1,0:T(8,128)S(1)} %constant_dynamic-slice_fusion), channel_id=1, source_target_pairs={{0,16},{1,17},{2,18},{3,19},{4,20},{5,21},{6,22},{7,23},{8,24},{9,... | collective-permute-start | bytes 98312 | tf_op jit(solution)/shard_map/ppermute | solution.py:97
  68.8 5.0 %all-to-all-done = f32[32,16,128]{2,1,0:T(8,128)S(1)} async-done(((f32[32,16,128]{2,1,0:T(8,128)}), f32[32,16,128]{2,1,0:T(8,128)S(1)}, u32[]{:S(2)}, u32[]{:S(2)}) %all-to-all-start) | async-done | bytes 262176 | tf_op jit(solution)/shard_map/all_to_all | solution.py:110
  73.8 0.6 copy_bitcast_fusion
  (30 shorter events, 0.6 us)
Async XLA Ops:
  0.7 9.4 %collective-permute-start = (bf16[1,4,16,128]{3,1,2,0:T(4,128)(2,1)S(1)}, bf16[1,4,16,128]{3,1,2,0:T(4,128)(2,1)S(1)}, u32[]{:S(2)}, u32[]{:S(2)}) collective-permute-start(bf16[1,4,16,128]{3,1,2,0:T(4,128)(2,1)S(1)} %bitcast.95), channel_id=1, source_target_pairs={{0,128},{32,160},{64,192},{96,224},{128,0},{160,32},{192,64},{224,... | collective-permute-start | bytes 49160 | tf_op jit(solution)/shard_map/ppermute | solution.py:79
  3.9 6.2 %collective-permute-start.8 = (bf16[1,4,16,128]{3,1,2,0:T(4,128)(2,1)S(1)}, bf16[1,4,16,128]{3,1,2,0:T(4,128)(2,1)S(1)}, u32[]{:S(2)}, u32[]{:S(2)}) collective-permute-start(bf16[1,4,16,128]{3,1,2,0:T(4,128)(2,1)S(1)} %bitcast.96), channel_id=1, source_target_pairs={{0,16},{1,17},{2,18},{3,19},{4,20},{5,21},{6,22},{7,23},{8,24},{9,... | collective-permute-start | bytes 49160 | tf_op jit(solution)/shard_map/ppermute | solution.py:79
  10.2 4.0 %collective-permute-start.1 = (bf16[2,4,16,128]{3,1,2,0:T(4,128)(2,1)S(1)}, bf16[2,4,16,128]{3,1,2,0:T(4,128)(2,1)S(1)}, u32[]{:S(2)}, u32[]{:S(2)}) collective-permute-start(bf16[2,4,16,128]{3,1,2,0:T(4,128)(2,1)S(1)} %get-tuple-element.7), channel_id=1, source_target_pairs={{0,64},{32,96},{64,0},{96,32},{128,192},{160,224},{192,128},{224,1... | collective-permute-start | bytes 98312 | tf_op jit(solution)/shard_map/ppermute | solution.py:79
  14.2 4.4 %collective-permute-start.2 = (bf16[4,4,16,128]{3,2,1,0:T(8,128)(2,1)S(1)}, bf16[4,4,16,128]{3,2,1,0:T(8,128)(2,1)S(1)}, u32[]{:S(2)}, u32[]{:S(2)}) collective-permute-start(bf16[4,4,16,128]{3,2,1,0:T(8,128)(2,1)S(1)} %bitcast.102), channel_id=1, source_target_pairs={{0,32},{32,0},{64,96},{96,64},{128,160},{160,128},{192,224},{224,1... | collective-permute-start | bytes 196616 | tf_op jit(solution)/shard_map/ppermute | solution.py:79
  27.6 6.7 %collective-permute-start.3 = (f32[16,4,16,128]{3,2,1,0:T(8,128)S(1)}, f32[16,4,16,128]{3,2,1,0:T(8,128)S(1)}, u32[]{:S(2)}, u32[]{:S(2)}) collective-permute-start(f32[16,4,16,128]{3,2,1,0:T(8,128)S(1)} %dynamic-slice_bitcast_fusion), channel_id=1, source_target_pairs={{0,1},{1,0},{2,3},{3,2},{4,5},{5,4},{6,7},{7,6},{8,9},{9,8},{10,11... | collective-permute-start | bytes 1572872 | tf_op jit(solution)/shard_map/ppermute | solution.py:97
  28.8 8.2 %collective-permute-start.9 = (bf16[2,4,16,128]{3,1,2,0:T(4,128)(2,1)S(1)}, bf16[2,4,16,128]{3,1,2,0:T(4,128)(2,1)S(1)}, u32[]{:S(2)}, u32[]{:S(2)}) collective-permute-start(bf16[2,4,16,128]{3,1,2,0:T(4,128)(2,1)S(1)} %get-tuple-element.8), channel_id=1, source_target_pairs={{0,12},{1,13},{2,14},{3,15},{4,8},{5,9},{6,10},{7,11},{8,4},{9,5},... | collective-permute-start | bytes 98312 | tf_op jit(solution)/shard_map/ppermute | solution.py:79
  35.4 10.5 %collective-permute-start.4 = (f32[8,4,16,128]{3,2,1,0:T(8,128)S(1)}, f32[8,4,16,128]{3,2,1,0:T(8,128)S(1)}, u32[]{:S(2)}, u32[]{:S(2)}) collective-permute-start(f32[8,4,16,128]{3,2,1,0:T(8,128)S(1)} %dynamic-slice_bitcast_fusion.1), channel_id=1, source_target_pairs={{0,2},{1,3},{2,0},{3,1},{4,6},{5,7},{6,4},{7,5},{8,10},{9,11},{10,... | collective-permute-start | bytes 786440 | tf_op jit(solution)/shard_map/ppermute | solution.py:97
  37.1 8.7 %collective-permute-start.10 = (bf16[4,4,16,128]{3,2,1,0:T(8,128)(2,1)S(1)}, bf16[4,4,16,128]{3,2,1,0:T(8,128)(2,1)S(1)}, u32[]{:S(2)}, u32[]{:S(2)}) collective-permute-start(bf16[4,4,16,128]{3,2,1,0:T(8,128)(2,1)S(1)} %bitcast.100), channel_id=1, source_target_pairs={{0,4},{1,5},{2,6},{3,7},{4,0},{5,1},{6,2},{7,3},{8,12},{9,13},{10,... | collective-permute-start | bytes 196616 | tf_op jit(solution)/shard_map/ppermute | solution.py:79
  45.8 6.0 %collective-permute-start.11 = (bf16[8,4,16,128]{3,2,1,0:T(8,128)(2,1)S(1)}, bf16[8,4,16,128]{3,2,1,0:T(8,128)(2,1)S(1)}, u32[]{:S(2)}, u32[]{:S(2)}) collective-permute-start(bf16[8,4,16,128]{3,2,1,0:T(8,128)(2,1)S(1)} %bitcast.91), channel_id=1, source_target_pairs={{0,2},{1,3},{2,0},{3,1},{4,6},{5,7},{6,4},{7,5},{8,10},{9,11},{10,... | collective-permute-start | bytes 393224 | tf_op jit(solution)/shard_map/ppermute | solution.py:79
  46.0 7.7 %collective-permute-start.5 = (f32[4,4,16,128]{3,2,1,0:T(8,128)S(1)}, f32[4,4,16,128]{3,2,1,0:T(8,128)S(1)}, u32[]{:S(2)}, u32[]{:S(2)}) collective-permute-start(f32[4,4,16,128]{3,2,1,0:T(8,128)S(1)} %dynamic-slice_bitcast_fusion.2), channel_id=1, source_target_pairs={{0,4},{1,5},{2,6},{3,7},{4,0},{5,1},{6,2},{7,3},{8,12},{9,13},{10,... | collective-permute-start | bytes 393224 | tf_op jit(solution)/shard_map/ppermute | solution.py:97
  51.8 5.0 %collective-permute-start.12 = (bf16[16,4,16,128]{3,2,1,0:T(8,128)(2,1)S(1)}, bf16[16,4,16,128]{3,2,1,0:T(8,128)(2,1)S(1)}, u32[]{:S(2)}, u32[]{:S(2)}) collective-permute-start(bf16[16,4,16,128]{3,2,1,0:T(8,128)(2,1)S(1)} %bitcast.88), channel_id=1, source_target_pairs={{0,1},{1,0},{2,3},{3,2},{4,5},{5,4},{6,7},{7,6},{8,9},{9,8},{10,11... | collective-permute-start | bytes 786440 | tf_op jit(solution)/shard_map/ppermute | solution.py:79
  53.8 12.8 %collective-permute-start.6 = (f32[2,4,16,128]{3,2,1,0:T(8,128)S(1)}, f32[2,4,16,128]{3,2,1,0:T(8,128)S(1)}, u32[]{:S(2)}, u32[]{:S(2)}) collective-permute-start(f32[2,4,16,128]{3,2,1,0:T(8,128)S(1)} %dynamic-slice_bitcast_fusion.3), channel_id=1, source_target_pairs={{0,12},{1,13},{2,14},{3,15},{4,8},{5,9},{6,10},{7,11},{8,4},{9,5},... | collective-permute-start | bytes 196616 | tf_op jit(solution)/shard_map/ppermute | solution.py:97
  63.2 10.6 %all-to-all-start = ((f32[32,16,128]{2,1,0:T(8,128)}), f32[32,16,128]{2,1,0:T(8,128)S(1)}, u32[]{:S(2)}, u32[]{:S(2)}) async-start(f32[32,16,128]{2,1,0:T(8,128)} %shard_map.83), calls=%async_computation | async-start | bytes 524288 | tf_op jit(solution)/shard_map/all_to_all | solution.py:110
  66.6 7.2 %collective-permute-start.7 = (f32[1,4,16,128]{3,2,1,0:T(8,128)S(1)}, f32[1,4,16,128]{3,2,1,0:T(8,128)S(1)}, u32[]{:S(2)}, u32[]{:S(2)}) collective-permute-start(f32[1,4,16,128]{3,2,1,0:T(8,128)S(1)} %constant_dynamic-slice_fusion), channel_id=1, source_target_pairs={{0,16},{1,17},{2,18},{3,19},{4,20},{5,21},{6,22},{7,23},{8,24},{9,... | collective-permute-start | bytes 98312 | tf_op jit(solution)/shard_map/ppermute | solution.py:97
